TPU v7x, 256 devices: a whole 4x4x8 slice. The times are simulated.
256 devices in a mesh: rep: 4 (over z_hi, core), ep: 64 (over z_lo, y, x).
Axes of the slice: x: 4, y: 4, z: 8 (z_hi: 2, z_lo: 4; z = z_hi * 4 + z_lo), core: 2. Of those that a mesh axis runs over, the one named last changes fastest.
Arguments:
- tokens: bfloat16 [4096, 3584], P('ep', 'rep'), may hold values from -6 to 6
- route_ids: int32 [4096, 8], P('ep'), may hold values from 0 to 127, all different within a row; in each aligned block of 64 rows (0 to 63, 64 to 127, ...) at most 6 rows name the same one
- route_weights: float32 [4096, 8], P('ep'), may hold values from 0.05 to 0.5
- swap_plan: int32 [64, 2], replicated, may hold values from 0 to 63, as said below
- gate_up: bfloat16 [128, 3584, 2, 1024], P('ep', None, None, 'rep'), may hold values from -0.09375 to 0.09375
- down: bfloat16 [128, 1024, 3584], P('ep', 'rep'), may hold values from -0.1875 to 0.1875
Outputs:
- mixed: bfloat16 [4096, 3584], P('ep', 'rep')
Inputs may be any that keep to these rules, and one draw needn't show every extreme that they name: swap_plan[d, 0] is d or the index 32 away from d (d + 64 / 2 modulo 64), and the pairing is mutual; swap_plan[d, 1] is a local slot below 2; at least one pair swaps. `route_ids`: each row names 8 different slots; among the rows of one index of ep no slot is named by more than 6 rows, a bound that some blocks reach.
All inputs are finite; a program needn't handle non-finite values.
Results may differ from a plain program's by a relative error of at most 0.012.
Values may be sent and summed in bfloat16 or wider, within the bound.
No kernel may reach another device: no remote copies, remote signals or barrier semaphores. Data moves between devices by JAX's collectives and lax.ppermute only.
A program may use at most 128 MiB of HBM per device.

v0:
```python
import jax
import jax.numpy as jnp
import numpy as np
from jax import lax
from jax.sharding import Mesh
from jax.sharding import PartitionSpec as P

EP_AXES = ("z", "y", "x")
REP_AXES = ("zh", "core")
RING = ("zh", "z")
PLANE = ("y", "x")


def pair_swap(value, axis):
    return lax.ppermute(value, axis, [(0, 1), (1, 0)])


def ring_shift(value, shift):
    size = lax.axis_size(RING)
    return lax.ppermute(value, RING, [(i, (i + shift) % size) for i in range(size)])


def plane_a2a(value):
    return lax.all_to_all(value, PLANE, 0, 0, tiled=True)


def ring_out(chunks):
    cut = chunks.shape[1] // 2
    far = jnp.concatenate([ring_shift(chunks[2, :cut], 2), ring_shift(chunks[2, cut:], -2)])
    return jnp.stack([chunks[0], ring_shift(chunks[1], 1), far, ring_shift(chunks[3], -1)])


def ring_back(chunks):
    cut = chunks.shape[1] // 2
    far = jnp.concatenate([ring_shift(chunks[2, :cut], -2), ring_shift(chunks[2, cut:], 2)])
    return jnp.stack([chunks[0], ring_shift(chunks[1], -1), far, ring_shift(chunks[3], 1)])


def pick(flag, first, second):
    return jnp.where(flag, first, second), jnp.where(flag, second, first)


def holder_of(swap_plan, exp_dev):
    ep_size = swap_plan.shape[0]
    slot = jnp.arange(ep_size * exp_dev, dtype=jnp.int32)
    partner = jnp.repeat(swap_plan[:, 0], exp_dev)
    given = jnp.repeat(swap_plan[:, 1], exp_dev)
    choose = (partner[:, None] == jnp.arange(ep_size, dtype=jnp.int32)[None, :]).astype(jnp.float32)
    partner_given = jnp.dot(choose, swap_plan[:, 1].astype(jnp.float32)).astype(jnp.int32)
    moved = (partner != slot // exp_dev) & (slot % exp_dev == given)
    return jnp.where(moved, partner * exp_dev + partner_given, slot)


def shards(tokens, route_ids, route_weights, swap_plan, gate_up, down):
    n_z = lax.axis_size("z")
    n_plane = lax.axis_size("y") * lax.axis_size("x")
    ep_size = n_z * n_plane
    core = lax.axis_index("core")
    half = lax.axis_index("zh")
    exp_dev = gate_up.shape[0]
    experts = exp_dev * ep_size
    tok_dev, top_k = route_ids.shape
    routed = tok_dev * top_k
    capacity = max(2, (routed * 3 + 2 * experts - 1) // (2 * experts))
    places = experts * capacity
    width = tokens.shape[1]
    cut = [slice(i * width, (i + 1) * width) for i in range(4)]

    holder = holder_of(swap_plan, exp_dev)
    catalog = jnp.arange(experts, dtype=jnp.int32)
    named = (route_ids.reshape(routed)[:, None] == catalog[None, :]).astype(jnp.float32)
    owners = jnp.dot(named, holder.astype(jnp.float32)).astype(jnp.int32)
    one_hot = (owners[:, None] == catalog[None, :]).astype(jnp.float32)
    earlier = (jnp.arange(routed)[:, None] > jnp.arange(routed)[None, :]).astype(jnp.float32)
    before = jnp.dot(earlier, one_hot, preferred_element_type=jnp.float32)
    position = jnp.sum(before * one_hot, axis=1).astype(jnp.int32)
    device = owners // exp_dev
    plane = device % n_plane
    offset = (device // n_plane - lax.axis_index("z")) % n_z
    slot = owners % exp_dev
    rank = jnp.where(slot == 0, plane * n_z + offset, offset * n_plane + plane)
    place = (slot * n_z * n_plane + rank) * capacity + position
    hits = (place[:, None] == jnp.arange(places, dtype=jnp.int32)[None, :]).reshape(tok_dev, top_k, places)
    gather = jnp.sum(hits.astype(jnp.bfloat16), axis=1)
    mixing = jnp.sum(jnp.where(hits, route_weights[:, :, None], 0.0), axis=1)

    other = pair_swap(tokens, "zh")
    low, high = pick(half == 0, tokens, other)
    features = jnp.concatenate([low, high], axis=1)
    outgoing = lax.dot_general(
        gather, features, (((0,), (0,)), ((), ())), preferred_element_type=jnp.float32
    ).astype(jnp.bfloat16)

    half_rows = places // exp_dev
    wide = 2 * width
    first = outgoing[:half_rows].reshape(n_plane, half_rows // n_plane, wide)
    second = outgoing[half_rows:].reshape(n_z, half_rows // n_z, wide)
    first = plane_a2a(first)
    second = ring_out(second)
    first = first.reshape(n_plane, n_z, capacity, wide).transpose(1, 0, 2, 3)
    second = second.reshape(n_z, n_plane, capacity, wide).transpose(1, 0, 2, 3)
    first = ring_out(first.reshape(n_z, half_rows // n_z, wide))
    second = plane_a2a(second.reshape(n_plane, half_rows // n_plane, wide))
    arrived = [first.reshape(half_rows, wide), second.reshape(half_rows, wide)]

    mine = jnp.stack(arrived)
    theirs = pair_swap(mine, "core")
    even, odd = pick(core == 0, mine, theirs)
    rows = jnp.concatenate(
        [even[..., :width], odd[..., :width], even[..., width:], odd[..., width:]], axis=-1
    )
    projected = jnp.einsum("srd,sdgf->srgf", rows, gate_up, preferred_element_type=jnp.float32)
    hidden = (jax.nn.silu(projected[:, :, 0]) * projected[:, :, 1]).astype(jnp.bfloat16)
    partial = jnp.einsum("srf,sfd->srd", hidden, down, preferred_element_type=jnp.float32).astype(
        jnp.bfloat16
    )
    part_even = jnp.concatenate([partial[..., cut[0]], partial[..., cut[2]]], axis=-1)
    part_odd = jnp.concatenate([partial[..., cut[1]], partial[..., cut[3]]], axis=-1)
    keep, send = pick(core == 0, part_even, part_odd)
    paired = (keep.astype(jnp.float32) + pair_swap(send, "core").astype(jnp.float32)).astype(jnp.bfloat16)

    first = ring_back(paired[0].reshape(n_z, half_rows // n_z, wide))
    second = plane_a2a(paired[1].reshape(n_plane, half_rows // n_plane, wide))
    first = first.reshape(n_z, n_plane, capacity, wide).transpose(1, 0, 2, 3)
    second = second.reshape(n_plane, n_z, capacity, wide).transpose(1, 0, 2, 3)
    first = plane_a2a(first.reshape(n_plane, half_rows // n_plane, wide))
    second = ring_back(second.reshape(n_z, half_rows // n_z, wide))
    returned = jnp.concatenate([first.reshape(half_rows, wide), second.reshape(half_rows, wide)])
    weighted = jnp.dot(
        mixing,
        returned.astype(jnp.float32),
        precision=lax.Precision.HIGHEST,
        preferred_element_type=jnp.float32,
    )
    own, away = pick(half == 0, weighted[:, :width], weighted[:, width:])
    return (own + pair_swap(away.astype(jnp.bfloat16), "zh").astype(jnp.float32)).astype(jnp.bfloat16)


def solution(mesh):
    rep_size, ep_size = mesh.devices.shape
    side = round(ep_size ** (1 / 3))
    shape = (2, rep_size // 2, side, side, side)
    grid = Mesh(np.asarray(mesh.devices).reshape(shape), REP_AXES + EP_AXES)
    return jax.shard_map(
        shards,
        mesh=grid,
        in_specs=(
            P(EP_AXES, REP_AXES),
            P(EP_AXES, None),
            P(EP_AXES, None),
            P(),
            P(EP_AXES, None, None, REP_AXES),
            P(EP_AXES, REP_AXES, None),
        ),
        out_specs=P(EP_AXES, REP_AXES),
        check_vma=False,
    )
```

profile of v0, /device:TPU:2, one launch (start us, length us, event | category | flops | bytes accessed | tf_op | source)
XLA Modules:
  0.0 182.1 jit_solution(6653626261366316798)
XLA Ops:
  0.0 7.2 %collective-permute-start = (bf16[64,896]{1,0:T(8,128)(2,1)}, bf16[64,896]{1,0:T(8,128)(2,1)S(1)}, u32[]{:S(2)}, u32[]{:S(2)}) collective-permute-start(bf16[64,896]{1,0:T(8,128)(2,1)} %param.6), channel_id=1, source_target_pairs={{0,128},{128,0},{1,129},{129,1},{2,130},{130,2},{3,131},{131,3},{4... | collective-permute-start | bytes 344072 | tf_op jit(solution)/shard_map/ppermute | solution.py:15
  13.1 1.7 fusion.64
  14.8 7.5 %all-to-all-start = ((bf16[16,24,1792]{2,1,0:T(8,128)(2,1)}), bf16[16,24,1792]{2,1,0:T(8,128)(2,1)}, u32[]{:S(2)}, u32[]{:S(2)}) async-start(bf16[16,24,1792]{2,1,0:T(8,128)(2,1)} %bitcast.116), calls=%async_computation | async-start | bytes 2752512 | tf_op jit(solution)/shard_map/all_to_all | solution.py:24
  22.3 1.8 slice_bitcast_fusion.7
  24.1 3.6 %collective-permute-start.6 = (bf16[48,1792]{1,0:T(8,128)(2,1)}, bf16[48,1792]{1,0:T(8,128)(2,1)}, u32[]{:S(2)}, u32[]{:S(2)}) collective-permute-start(bf16[48,1792]{1,0:T(8,128)(2,1)} %get-tuple-element.37), channel_id=1, source_target_pairs={{0,32},{16,48},{32,128},{48,144},{128,160},{144,176},{160,0},{176,... | collective-permute-start | bytes 516104 | tf_op jit(solution)/shard_map/ppermute | solution.py:20
  27.7 2.8 %collective-permute-start.7 = (bf16[48,1792]{1,0:T(8,128)(2,1)}, bf16[48,1792]{1,0:T(8,128)(2,1)}, u32[]{:S(2)}, u32[]{:S(2)}) collective-permute-start(bf16[48,1792]{1,0:T(8,128)(2,1)} %get-tuple-element.38), channel_id=1, source_target_pairs={{0,160},{16,176},{32,0},{48,16},{128,32},{144,48},{160,128},{176,1... | collective-permute-start | bytes 516104 | tf_op jit(solution)/shard_map/ppermute | solution.py:20
  31.8 2.7 %collective-permute-start.8 = (bf16[96,1792]{1,0:T(8,128)(2,1)S(1)}, bf16[96,1792]{1,0:T(8,128)(2,1)S(1)}, u32[]{:S(2)}, u32[]{:S(2)}) collective-permute-start(bf16[96,1792]{1,0:T(8,128)(2,1)S(1)} %get-tuple-element.23), channel_id=1, source_target_pairs={{0,176},{16,0},{32,16},{48,32},{128,48},{144,128},{160,144},{176,1... | collective-permute-start | bytes 1032200 | tf_op jit(solution)/shard_map/ppermute | solution.py:20
  34.7 3.8 %collective-permute-done.6 = bf16[48,1792]{1,0:T(8,128)(2,1)} collective-permute-done((bf16[48,1792]{1,0:T(8,128)(2,1)}, bf16[48,1792]{1,0:T(8,128)(2,1)}, u32[]{:S(2)}, u32[]{:S(2)}) %collective-permute-start.6) | collective-permute-done | bytes 172064 | tf_op jit(solution)/shard_map/ppermute | solution.py:20
  39.6 4.3 %collective-permute-done.5 = bf16[96,1792]{1,0:T(8,128)(2,1)S(1)} collective-permute-done((bf16[96,1792]{1,0:T(8,128)(2,1)}, bf16[96,1792]{1,0:T(8,128)(2,1)S(1)}, u32[]{:S(2)}, u32[]{:S(2)}) %collective-permute-start.5) | collective-permute-done | bytes 344096 | tf_op jit(solution)/shard_map/ppermute | solution.py:20
  45.8 1.5 copy.86
  47.3 7.2 %all-to-all-start.1 = ((bf16[16,24,1792]{2,1,0:T(8,128)(2,1)}), bf16[16,24,1792]{2,1,0:T(8,128)(2,1)S(1)}, u32[]{:S(2)}, u32[]{:S(2)}) async-start(bf16[16,24,1792]{2,1,0:T(8,128)(2,1)} %copy.86), calls=%async_computation.1 | async-start | bytes 2752512 | tf_op jit(solution)/shard_map/all_to_all | solution.py:24
  54.6 1.6 copy.78
  60.4 3.0 %collective-permute-start.3 = (bf16[48,1792]{1,0:T(8,128)(2,1)}, bf16[48,1792]{1,0:T(8,128)(2,1)}, u32[]{:S(2)}, u32[]{:S(2)}) collective-permute-start(bf16[48,1792]{1,0:T(8,128)(2,1)} %bitcast.105), channel_id=1, source_target_pairs={{0,160},{16,176},{32,0},{48,16},{128,32},{144,48},{160,128},{176,1... | collective-permute-start | bytes 516104 | tf_op jit(solution)/shard_map/ppermute | solution.py:20
  64.2 3.2 %collective-permute-start.4 = (bf16[96,1792]{1,0:T(8,128)(2,1)S(1)}, bf16[96,1792]{1,0:T(8,128)(2,1)}, u32[]{:S(2)}, u32[]{:S(2)}) collective-permute-start(bf16[96,1792]{1,0:T(8,128)(2,1)S(1)} %squeeze.62), channel_id=1, source_target_pairs={{0,176},{16,0},{32,16},{48,32},{128,48},{144,128},{160,144},{176,1... | collective-permute-start | bytes 1032200 | tf_op jit(solution)/shard_map/ppermute | solution.py:20
  67.6 3.8 %collective-permute-done.2 = bf16[48,1792]{1,0:T(8,128)(2,1)S(1)} collective-permute-done((bf16[48,1792]{1,0:T(8,128)(2,1)}, bf16[48,1792]{1,0:T(8,128)(2,1)S(1)}, u32[]{:S(2)}, u32[]{:S(2)}) %collective-permute-start.2) | collective-permute-done | bytes 172064 | tf_op jit(solution)/shard_map/ppermute | solution.py:20
  73.2 2.0 %collective-permute-done.1 = bf16[96,1792]{1,0:T(8,128)(2,1)} collective-permute-done((bf16[96,1792]{1,0:T(8,128)(2,1)S(1)}, bf16[96,1792]{1,0:T(8,128)(2,1)}, u32[]{:S(2)}, u32[]{:S(2)}) %collective-permute-start.1) | collective-permute-done | bytes 344096 | tf_op jit(solution)/shard_map/ppermute | solution.py:20
  75.2 1.5 collective-permute-done.4
  76.7 1.3 pad_maximum_fusion.3
  78.0 1.8 pad_maximum_fusion
  79.7 5.4 %collective-permute-done.9 = bf16[2,384,1792]{2,1,0:T(8,128)(2,1)} collective-permute-done((bf16[2,384,1792]{2,1,0:T(8,128)(2,1)}, bf16[2,384,1792]{2,1,0:T(8,128)(2,1)}, u32[]{:S(2)}, u32[]{:S(2)}) %collective-permute-start.9) | collective-permute-done | bytes 2752544 | tf_op jit(solution)/shard_map/ppermute | solution.py:15
  85.2 2.1 %broadcast_select_fusion.2 = (bf16[2,384,1792]{2,1,0:T(8,128)(2,1)S(1)}, bf16[2,384,1792]{2,1,0:T(8,128)(2,1)S(1)}) fusion(bf16[2,384,1792]{2,1,0:T(8,128)(2,1)} %collective-permute-done.9, pred[]{:T(512)S(6)} %eq.95, bf16[1,384,1792]{2,1,0:T(8,128)(2,1)S(1)} %bitcast.108, bf16[1,384,1792]{2,1,0:T(8,128)(2,1)S(1)} %bitcast.110), kind=kLoop, calls=%fused_computation.21 | loop fusion | flops 4128768 | bytes 11010049 | tf_op jit(solution)/shard_map/jit(_where)/select_n | solution.py:40
  88.2 1.2 slice-done.1
  89.4 3.3 %fusion = f32[2,384,2,256]{3,1,2,0:T(8,128)S(1)} fusion(bf16[2,3584,2,256]{3,2,1,0:T(2,128)(2,1)S(1)} %bitcast.129, bf16[2,384,896]{2,1,0:T(8,128)(2,1)S(1)} %get-tuple-element.43, bf16[2,384,896]{2,1,0:T(8,128)(2,1)S(1)} %get-tuple-element.17, bf16[2,384,896]{2,1,0:T(8,128)(2,1)S(1)} %get-tuple-element.44, bf16[2,384,896]{2,1,0:T(8,128)(2,1)S(1)} %get-tuple-element.16), kind=kOutput, calls=%fused_computation | convolution fusion | flops 2840592384 | bytes 14417920 | tf_op jit(solution)/shard_map/srd,sdgf->srgf/dot_general | solution.py:112
  92.7 1.6 convolution_convert_fusion
  96.0 5.0 %collective-permute-done.10 = bf16[2,384,1792]{2,1,0:T(8,128)(2,1)S(1)} collective-permute-done((bf16[2,384,1792]{2,1,0:T(8,128)(2,1)S(1)}, bf16[2,384,1792]{2,1,0:T(8,128)(2,1)S(1)}, u32[]{:S(2)}, u32[]{:S(2)}) %collective-permute-start.10) | collective-permute-done | bytes 2752544 | tf_op jit(solution)/shard_map/ppermute | solution.py:15
  101.0 1.1 add_convert_fusion
  102.1 1.7 fusion.61
  103.9 7.2 %all-to-all-start.3 = ((bf16[16,24,1792]{2,1,0:T(8,128)(2,1)}), bf16[16,24,1792]{2,1,0:T(8,128)(2,1)}, u32[]{:S(2)}, u32[]{:S(2)}) async-start(bf16[16,24,1792]{2,1,0:T(8,128)(2,1)} %bitcast.115), calls=%async_computation.3 | async-start | bytes 2752512 | tf_op jit(solution)/shard_map/all_to_all | solution.py:24
  111.1 1.8 slice_bitcast_fusion.5
  112.9 3.2 %collective-permute-start.12 = (bf16[48,1792]{1,0:T(8,128)(2,1)}, bf16[48,1792]{1,0:T(8,128)(2,1)}, u32[]{:S(2)}, u32[]{:S(2)}) collective-permute-start(bf16[48,1792]{1,0:T(8,128)(2,1)} %get-tuple-element.25), channel_id=1, source_target_pairs={{0,160},{16,176},{32,0},{48,16},{128,32},{144,48},{160,128},{176,1... | collective-permute-start | bytes 516104 | tf_op jit(solution)/shard_map/ppermute | solution.py:20
  116.9 4.7 %collective-permute-start.11 = (bf16[96,1792]{1,0:T(8,128)(2,1)}, bf16[96,1792]{1,0:T(8,128)(2,1)S(1)}, u32[]{:S(2)}, u32[]{:S(2)}) collective-permute-start(bf16[96,1792]{1,0:T(8,128)(2,1)} %get-tuple-element.13), channel_id=1, source_target_pairs={{0,176},{16,0},{32,16},{48,32},{128,48},{144,128},{160,144},{176,1... | collective-permute-start | bytes 1032200 | tf_op jit(solution)/shard_map/ppermute | solution.py:20
  121.9 2.7 %collective-permute-done.12 = bf16[48,1792]{1,0:T(8,128)(2,1)} collective-permute-done((bf16[48,1792]{1,0:T(8,128)(2,1)}, bf16[48,1792]{1,0:T(8,128)(2,1)}, u32[]{:S(2)}, u32[]{:S(2)}) %collective-permute-start.12) | collective-permute-done | bytes 172064 | tf_op jit(solution)/shard_map/ppermute | solution.py:20
  124.6 4.3 %collective-permute-done.13 = bf16[48,1792]{1,0:T(8,128)(2,1)} collective-permute-done((bf16[48,1792]{1,0:T(8,128)(2,1)}, bf16[48,1792]{1,0:T(8,128)(2,1)}, u32[]{:S(2)}, u32[]{:S(2)}) %collective-permute-start.13) | collective-permute-done | bytes 172064 | tf_op jit(solution)/shard_map/ppermute | solution.py:20
  130.0 1.9 %collective-permute-done.11 = bf16[96,1792]{1,0:T(8,128)(2,1)S(1)} collective-permute-done((bf16[96,1792]{1,0:T(8,128)(2,1)}, bf16[96,1792]{1,0:T(8,128)(2,1)S(1)}, u32[]{:S(2)}, u32[]{:S(2)}) %collective-permute-start.11) | collective-permute-done | bytes 344096 | tf_op jit(solution)/shard_map/ppermute | solution.py:20
  132.0 3.4 %collective-permute-done.14 = bf16[96,1792]{1,0:T(8,128)(2,1)S(1)} collective-permute-done((bf16[96,1792]{1,0:T(8,128)(2,1)S(1)}, bf16[96,1792]{1,0:T(8,128)(2,1)S(1)}, u32[]{:S(2)}, u32[]{:S(2)}) %collective-permute-start.14) | collective-permute-done | bytes 344096 | tf_op jit(solution)/shard_map/ppermute | solution.py:20
  136.2 1.5 copy.90
  137.8 7.2 %all-to-all-start.2 = ((bf16[16,24,1792]{2,1,0:T(8,128)(2,1)}), bf16[16,24,1792]{2,1,0:T(8,128)(2,1)S(1)}, u32[]{:S(2)}, u32[]{:S(2)}) async-start(bf16[16,24,1792]{2,1,0:T(8,128)(2,1)} %copy.90), calls=%async_computation.2 | async-start | bytes 2752512 | tf_op jit(solution)/shard_map/all_to_all | solution.py:24
  145.0 1.6 copy.91
  149.8 2.9 %collective-permute-start.17 = (bf16[48,1792]{1,0:T(8,128)(2,1)}, bf16[48,1792]{1,0:T(8,128)(2,1)}, u32[]{:S(2)}, u32[]{:S(2)}) collective-permute-start(bf16[48,1792]{1,0:T(8,128)(2,1)} %bitcast.103), channel_id=1, source_target_pairs={{0,32},{16,48},{32,128},{48,144},{128,160},{144,176},{160,0},{176,... | collective-permute-start | bytes 516104 | tf_op jit(solution)/shard_map/ppermute | solution.py:20
  153.0 1.2 collective-permute-start.15
  155.4 1.2 select_reduce_fusion
  158.0 2.9 %collective-permute-done.17 = bf16[48,1792]{1,0:T(8,128)(2,1)} collective-permute-done((bf16[48,1792]{1,0:T(8,128)(2,1)}, bf16[48,1792]{1,0:T(8,128)(2,1)}, u32[]{:S(2)}, u32[]{:S(2)}) %collective-permute-start.17) | collective-permute-done | bytes 172064 | tf_op jit(solution)/shard_map/ppermute | solution.py:20
  161.9 3.2 %collective-permute-done.15 = bf16[96,1792]{1,0:T(8,128)(2,1)S(1)} collective-permute-done((bf16[96,1792]{1,0:T(8,128)(2,1)S(1)}, bf16[96,1792]{1,0:T(8,128)(2,1)S(1)}, u32[]{:S(2)}, u32[]{:S(2)}) %collective-permute-start.15) | collective-permute-done | bytes 344096 | tf_op jit(solution)/shard_map/ppermute | solution.py:20
  165.1 3.1 %collective-permute-done.18 = bf16[96,1792]{1,0:T(8,128)(2,1)} collective-permute-done((bf16[96,1792]{1,0:T(8,128)(2,1)S(1)}, bf16[96,1792]{1,0:T(8,128)(2,1)}, u32[]{:S(2)}, u32[]{:S(2)}) %collective-permute-start.18) | collective-permute-done | bytes 344096 | tf_op jit(solution)/shard_map/ppermute | solution.py:20
  168.3 1.3 pad_maximum_fusion.4
  169.6 1.5 fusion.8
  171.1 3.1 %collective-permute-start.19 = (bf16[64,896]{1,0:T(8,128)(2,1)S(1)}, bf16[64,896]{1,0:T(8,128)(2,1)S(1)}, u32[]{:S(2)}, u32[]{:S(2)}) collective-permute-start(bf16[64,896]{1,0:T(8,128)(2,1)S(1)} %select_convert_fusion), channel_id=1, source_target_pairs={{0,128},{128,0},{1,129},{129,1},{2,130},{130,2},{3,131},{131,3},{4... | collective-permute-start | bytes 344072 | tf_op jit(solution)/shard_map/ppermute | solution.py:15
  174.2 7.2 %collective-permute-done.19 = bf16[64,896]{1,0:T(8,128)(2,1)S(1)} collective-permute-done((bf16[64,896]{1,0:T(8,128)(2,1)S(1)}, bf16[64,896]{1,0:T(8,128)(2,1)S(1)}, u32[]{:S(2)}, u32[]{:S(2)}) %collective-permute-start.19) | collective-permute-done | bytes 114720 | tf_op jit(solution)/shard_map/ppermute | solution.py:15
  (91 shorter events, 30.8 us)
Async XLA Ops:
  0.0 11.3 %collective-permute-start = (bf16[64,896]{1,0:T(8,128)(2,1)}, bf16[64,896]{1,0:T(8,128)(2,1)S(1)}, u32[]{:S(2)}, u32[]{:S(2)}) collective-permute-start(bf16[64,896]{1,0:T(8,128)(2,1)} %param.6), channel_id=1, source_target_pairs={{0,128},{128,0},{1,129},{129,1},{2,130},{130,2},{3,131},{131,3},{4... | collective-permute-start | bytes 344072 | tf_op jit(solution)/shard_map/ppermute | solution.py:15
  14.8 32.5 %all-to-all-start = ((bf16[16,24,1792]{2,1,0:T(8,128)(2,1)}), bf16[16,24,1792]{2,1,0:T(8,128)(2,1)}, u32[]{:S(2)}, u32[]{:S(2)}) async-start(bf16[16,24,1792]{2,1,0:T(8,128)(2,1)} %bitcast.116), calls=%async_computation | async-start | bytes 2752512 | tf_op jit(solution)/shard_map/all_to_all | solution.py:24
  24.1 14.3 %collective-permute-start.6 = (bf16[48,1792]{1,0:T(8,128)(2,1)}, bf16[48,1792]{1,0:T(8,128)(2,1)}, u32[]{:S(2)}, u32[]{:S(2)}) collective-permute-start(bf16[48,1792]{1,0:T(8,128)(2,1)} %get-tuple-element.37), channel_id=1, source_target_pairs={{0,32},{16,48},{32,128},{48,144},{128,160},{144,176},{160,0},{176,... | collective-permute-start | bytes 516104 | tf_op jit(solution)/shard_map/ppermute | solution.py:20
  27.7 10.7 %collective-permute-start.7 = (bf16[48,1792]{1,0:T(8,128)(2,1)}, bf16[48,1792]{1,0:T(8,128)(2,1)}, u32[]{:S(2)}, u32[]{:S(2)}) collective-permute-start(bf16[48,1792]{1,0:T(8,128)(2,1)} %get-tuple-element.38), channel_id=1, source_target_pairs={{0,160},{16,176},{32,0},{48,16},{128,32},{144,48},{160,128},{176,1... | collective-permute-start | bytes 516104 | tf_op jit(solution)/shard_map/ppermute | solution.py:20
  31.3 12.5 %collective-permute-start.5 = (bf16[96,1792]{1,0:T(8,128)(2,1)}, bf16[96,1792]{1,0:T(8,128)(2,1)S(1)}, u32[]{:S(2)}, u32[]{:S(2)}) collective-permute-start(bf16[96,1792]{1,0:T(8,128)(2,1)} %get-tuple-element.24), channel_id=1, source_target_pairs={{0,16},{16,32},{32,48},{48,128},{128,144},{144,160},{160,176},{176... | collective-permute-start | bytes 1032200 | tf_op jit(solution)/shard_map/ppermute | solution.py:20
  31.8 13.2 %collective-permute-start.8 = (bf16[96,1792]{1,0:T(8,128)(2,1)S(1)}, bf16[96,1792]{1,0:T(8,128)(2,1)S(1)}, u32[]{:S(2)}, u32[]{:S(2)}) collective-permute-start(bf16[96,1792]{1,0:T(8,128)(2,1)S(1)} %get-tuple-element.23), channel_id=1, source_target_pairs={{0,176},{16,0},{32,16},{48,32},{128,48},{144,128},{160,144},{176,1... | collective-permute-start | bytes 1032200 | tf_op jit(solution)/shard_map/ppermute | solution.py:20
  47.3 30.6 %all-to-all-start.1 = ((bf16[16,24,1792]{2,1,0:T(8,128)(2,1)}), bf16[16,24,1792]{2,1,0:T(8,128)(2,1)S(1)}, u32[]{:S(2)}, u32[]{:S(2)}) async-start(bf16[16,24,1792]{2,1,0:T(8,128)(2,1)} %copy.86), calls=%async_computation.1 | async-start | bytes 2752512 | tf_op jit(solution)/shard_map/all_to_all | solution.py:24
  58.6 12.8 %collective-permute-start.2 = (bf16[48,1792]{1,0:T(8,128)(2,1)}, bf16[48,1792]{1,0:T(8,128)(2,1)S(1)}, u32[]{:S(2)}, u32[]{:S(2)}) collective-permute-start(bf16[48,1792]{1,0:T(8,128)(2,1)} %bitcast.106), channel_id=1, source_target_pairs={{0,32},{16,48},{32,128},{48,144},{128,160},{144,176},{160,0},{176,... | collective-permute-start | bytes 516104 | tf_op jit(solution)/shard_map/ppermute | solution.py:20
  60.4 11.9 %collective-permute-start.3 = (bf16[48,1792]{1,0:T(8,128)(2,1)}, bf16[48,1792]{1,0:T(8,128)(2,1)}, u32[]{:S(2)}, u32[]{:S(2)}) collective-permute-start(bf16[48,1792]{1,0:T(8,128)(2,1)} %bitcast.105), channel_id=1, source_target_pairs={{0,160},{16,176},{32,0},{48,16},{128,32},{144,48},{160,128},{176,1... | collective-permute-start | bytes 516104 | tf_op jit(solution)/shard_map/ppermute | solution.py:20
  63.8 11.4 %collective-permute-start.1 = (bf16[96,1792]{1,0:T(8,128)(2,1)S(1)}, bf16[96,1792]{1,0:T(8,128)(2,1)}, u32[]{:S(2)}, u32[]{:S(2)}) collective-permute-start(bf16[96,1792]{1,0:T(8,128)(2,1)S(1)} %squeeze.59), channel_id=1, source_target_pairs={{0,16},{16,32},{32,48},{48,128},{128,144},{144,160},{160,176},{176... | collective-permute-start | bytes 1032200 | tf_op jit(solution)/shard_map/ppermute | solution.py:20
  64.2 12.5 %collective-permute-start.4 = (bf16[96,1792]{1,0:T(8,128)(2,1)S(1)}, bf16[96,1792]{1,0:T(8,128)(2,1)}, u32[]{:S(2)}, u32[]{:S(2)}) collective-permute-start(bf16[96,1792]{1,0:T(8,128)(2,1)S(1)} %squeeze.62), channel_id=1, source_target_pairs={{0,176},{16,0},{32,16},{48,32},{128,48},{144,128},{160,144},{176,1... | collective-permute-start | bytes 1032200 | tf_op jit(solution)/shard_map/ppermute | solution.py:20
  79.7 5.4 %collective-permute-start.9 = (bf16[2,384,1792]{2,1,0:T(8,128)(2,1)}, bf16[2,384,1792]{2,1,0:T(8,128)(2,1)}, u32[]{:S(2)}, u32[]{:S(2)}) collective-permute-start(bf16[2,384,1792]{2,1,0:T(8,128)(2,1)} %pad_maximum_fusion), channel_id=1, source_target_pairs={{0,64},{64,0},{1,65},{65,1},{2,66},{66,2},{3,67},{67,3},{4,68},{68... | collective-permute-start | bytes 8257544 | tf_op jit(solution)/shard_map/ppermute | solution.py:15
  85.2 3.0 %slice-start = ((s8[7340032]{0:T(1024)(128)(4,1)}), s8[4194304]{0:T(1024)(128)(4,1)S(1)}, s32[]{:S(2)}) async-start(s8[7340032]{0:T(1024)(128)(4,1)} %bitcast.128), calls=%async_computation.4 | async-start | bytes 8388608
  87.3 2.1 %slice-start.1 = ((s8[7340032]{0:T(1024)(128)(4,1)}), s8[3145728]{0:T(1024)(128)(4,1)S(1)}, s32[]{:S(2)}) async-start(s8[7340032]{0:T(1024)(128)(4,1)} %bitcast.128), calls=%async_computation.5 | async-start | bytes 6291456
  89.4 3.3 %copy-start = (bf16[2,256,3584]{2,1,0:T(8,128)(2,1)S(1)}, bf16[2,256,3584]{2,1,0:T(8,128)(2,1)}, u32[]{:S(2)}) copy-start(bf16[2,256,3584]{2,1,0:T(8,128)(2,1)} %param.11) | copy-start | bytes 11010052
  95.8 5.2 %collective-permute-start.10 = (bf16[2,384,1792]{2,1,0:T(8,128)(2,1)S(1)}, bf16[2,384,1792]{2,1,0:T(8,128)(2,1)S(1)}, u32[]{:S(2)}, u32[]{:S(2)}) collective-permute-start(bf16[2,384,1792]{2,1,0:T(8,128)(2,1)S(1)} %broadcast_select_fusion), channel_id=1, source_target_pairs={{0,64},{64,0},{1,65},{65,1},{2,66},{66,2},{3,67},{67,3},{4,68},{68... | collective-permute-start | bytes 8257544 | tf_op jit(solution)/shard_map/ppermute | solution.py:15
  103.9 33.9 %all-to-all-start.3 = ((bf16[16,24,1792]{2,1,0:T(8,128)(2,1)}), bf16[16,24,1792]{2,1,0:T(8,128)(2,1)}, u32[]{:S(2)}, u32[]{:S(2)}) async-start(bf16[16,24,1792]{2,1,0:T(8,128)(2,1)} %bitcast.115), calls=%async_computation.3 | async-start | bytes 2752512 | tf_op jit(solution)/shard_map/all_to_all | solution.py:24
  111.1 10.6 %copy-start.3 = (f32[64,8]{0,1:T(8,128)S(1)}, f32[64,8]{0,1:T(8,128)}, u32[]{:S(2)}) copy-start(f32[64,8]{0,1:T(8,128)} %param.8) | copy-start | bytes 6148
  112.9 11.7 %collective-permute-start.12 = (bf16[48,1792]{1,0:T(8,128)(2,1)}, bf16[48,1792]{1,0:T(8,128)(2,1)}, u32[]{:S(2)}, u32[]{:S(2)}) collective-permute-start(bf16[48,1792]{1,0:T(8,128)(2,1)} %get-tuple-element.25), channel_id=1, source_target_pairs={{0,160},{16,176},{32,0},{48,16},{128,32},{144,48},{160,128},{176,1... | collective-permute-start | bytes 516104 | tf_op jit(solution)/shard_map/ppermute | solution.py:20
  116.1 12.7 %collective-permute-start.13 = (bf16[48,1792]{1,0:T(8,128)(2,1)}, bf16[48,1792]{1,0:T(8,128)(2,1)}, u32[]{:S(2)}, u32[]{:S(2)}) collective-permute-start(bf16[48,1792]{1,0:T(8,128)(2,1)} %get-tuple-element.26), channel_id=1, source_target_pairs={{0,32},{16,48},{32,128},{48,144},{128,160},{144,176},{160,0},{176,... | collective-permute-start | bytes 516104 | tf_op jit(solution)/shard_map/ppermute | solution.py:20
  116.9 15.0 %collective-permute-start.11 = (bf16[96,1792]{1,0:T(8,128)(2,1)}, bf16[96,1792]{1,0:T(8,128)(2,1)S(1)}, u32[]{:S(2)}, u32[]{:S(2)}) collective-permute-start(bf16[96,1792]{1,0:T(8,128)(2,1)} %get-tuple-element.13), channel_id=1, source_target_pairs={{0,176},{16,0},{32,16},{48,32},{128,48},{144,128},{160,144},{176,1... | collective-permute-start | bytes 1032200 | tf_op jit(solution)/shard_map/ppermute | solution.py:20
  121.6 13.8 %collective-permute-start.14 = (bf16[96,1792]{1,0:T(8,128)(2,1)S(1)}, bf16[96,1792]{1,0:T(8,128)(2,1)S(1)}, u32[]{:S(2)}, u32[]{:S(2)}) collective-permute-start(bf16[96,1792]{1,0:T(8,128)(2,1)S(1)} %get-tuple-element.12), channel_id=1, source_target_pairs={{0,16},{16,32},{32,48},{48,128},{128,144},{144,160},{160,176},{176... | collective-permute-start | bytes 1032200 | tf_op jit(solution)/shard_map/ppermute | solution.py:20
  137.8 31.7 %all-to-all-start.2 = ((bf16[16,24,1792]{2,1,0:T(8,128)(2,1)}), bf16[16,24,1792]{2,1,0:T(8,128)(2,1)S(1)}, u32[]{:S(2)}, u32[]{:S(2)}) async-start(bf16[16,24,1792]{2,1,0:T(8,128)(2,1)} %copy.90), calls=%async_computation.2 | async-start | bytes 2752512 | tf_op jit(solution)/shard_map/all_to_all | solution.py:24
  149.1 8.9 %collective-permute-start.16 = (bf16[48,1792]{1,0:T(8,128)(2,1)}, bf16[48,1792]{1,0:T(8,128)(2,1)}, u32[]{:S(2)}, u32[]{:S(2)}) collective-permute-start(bf16[48,1792]{1,0:T(8,128)(2,1)} %bitcast.104), channel_id=1, source_target_pairs={{0,160},{16,176},{32,0},{48,16},{128,32},{144,48},{160,128},{176,1... | collective-permute-start | bytes 516104 | tf_op jit(solution)/shard_map/ppermute | solution.py:20
  149.8 11.1 %collective-permute-start.17 = (bf16[48,1792]{1,0:T(8,128)(2,1)}, bf16[48,1792]{1,0:T(8,128)(2,1)}, u32[]{:S(2)}, u32[]{:S(2)}) collective-permute-start(bf16[48,1792]{1,0:T(8,128)(2,1)} %bitcast.103), channel_id=1, source_target_pairs={{0,32},{16,48},{32,128},{48,144},{128,160},{144,176},{160,0},{176,... | collective-permute-start | bytes 516104 | tf_op jit(solution)/shard_map/ppermute | solution.py:20
  153.0 12.1 %collective-permute-start.15 = (bf16[96,1792]{1,0:T(8,128)(2,1)S(1)}, bf16[96,1792]{1,0:T(8,128)(2,1)S(1)}, u32[]{:S(2)}, u32[]{:S(2)}) collective-permute-start(bf16[96,1792]{1,0:T(8,128)(2,1)S(1)} %squeeze.71), channel_id=1, source_target_pairs={{0,176},{16,0},{32,16},{48,32},{128,48},{144,128},{160,144},{176,1... | collective-permute-start | bytes 1032200 | tf_op jit(solution)/shard_map/ppermute | solution.py:20
  154.4 13.9 %collective-permute-start.18 = (bf16[96,1792]{1,0:T(8,128)(2,1)S(1)}, bf16[96,1792]{1,0:T(8,128)(2,1)}, u32[]{:S(2)}, u32[]{:S(2)}) collective-permute-start(bf16[96,1792]{1,0:T(8,128)(2,1)S(1)} %squeeze.74), channel_id=1, source_target_pairs={{0,16},{16,32},{32,48},{48,128},{128,144},{144,160},{160,176},{176... | collective-permute-start | bytes 1032200 | tf_op jit(solution)/shard_map/ppermute | solution.py:20
  156.9 12.7 %copy-start.2 = (f32[64,768]{1,0:T(8,128)S(1)}, f32[64,768]{1,0:T(8,128)}, u32[]{:S(2)}) copy-start(f32[64,768]{1,0:T(8,128)} %select_reduce_fusion) | copy-start | bytes 589828
  165.1 3.1 %copy-start.1 = (bf16[96,1792]{1,0:T(8,128)(2,1)}, bf16[96,1792]{1,0:T(8,128)(2,1)S(1)}, u32[]{:S(2)}) copy-start(bf16[96,1792]{1,0:T(8,128)(2,1)S(1)} %collective-permute-done.15) | copy-start | bytes 1032196
  171.1 10.3 %collective-permute-start.19 = (bf16[64,896]{1,0:T(8,128)(2,1)S(1)}, bf16[64,896]{1,0:T(8,128)(2,1)S(1)}, u32[]{:S(2)}, u32[]{:S(2)}) collective-permute-start(bf16[64,896]{1,0:T(8,128)(2,1)S(1)} %select_convert_fusion), channel_id=1, source_target_pairs={{0,128},{128,0},{1,129},{129,1},{2,130},{130,2},{3,131},{131,3},{4... | collective-permute-start | bytes 344072 | tf_op jit(solution)/shard_map/ppermute | solution.py:15
where the time goes:
time: 183 us; the launch traced here: 182 us
  starting transfers between devices  69.9 us (38%)
  waiting for transfers between devices  57.4 us (31%)
  local copies, waits for them, and re-layouts  29.2 us (16%)
  other arithmetic  16.6 us (9%)
  matrix products  8.63 us (5%)
    ppermute x16, waiting for transfers between devices, ring_shift(): lax.ppermute(value, RING, [(i, (i + shift) % size) for i in range(size)])  39.7 us
    ppermute x16, starting transfers between devices, ring_shift(): lax.ppermute(value, RING, [(i, (i + shift) % size) for i in range(size)])  30.2 us
    all_to_all x4, starting transfers between devices, plane_a2a(): return lax.all_to_all(value, PLANE, 0, 0, tiled=True)  29.2 us
    ppermute x4, waiting for transfers between devices, pair_swap(): return lax.ppermute(value, axis, [(0, 1), (1, 0)])  17.6 us
    ppermute x4, starting transfers between devices, pair_swap(): return lax.ppermute(value, axis, [(0, 1), (1, 0)])  10.5 us
    unnamed x18, local copies, waits for them, and re-layouts  5.21 us
    select_n x3, other arithmetic, pick(): return (jnp.where(flag, first, second), jnp.where(flag, second, first))  3.73 us
  transfers between devices with their start and end apart: 24, of which 18 were waited for; matrix products, arithmetic and copies ran while one was open for 18% of the time, Pallas kernels for 0%

commit v1 on v0

--- a/solution.py
+++ b/solution.py
@@ -26,14 +26,19 @@
 
 def ring_out(chunks):
     cut = chunks.shape[1] // 2
-    far = jnp.concatenate([ring_shift(chunks[2, :cut], 2), ring_shift(chunks[2, cut:], -2)])
-    return jnp.stack([chunks[0], ring_shift(chunks[1], 1), far, ring_shift(chunks[3], -1)])
+    far = [ring_shift(chunks[2, :cut], 2), ring_shift(chunks[2, cut:], -2)]
+    return [chunks[0], ring_shift(chunks[1], 1), far, ring_shift(chunks[3], -1)]
 
 
 def ring_back(chunks):
     cut = chunks.shape[1] // 2
-    far = jnp.concatenate([ring_shift(chunks[2, :cut], -2), ring_shift(chunks[2, cut:], 2)])
-    return jnp.stack([chunks[0], ring_shift(chunks[1], -1), far, ring_shift(chunks[3], 1)])
+    far = [ring_shift(chunks[2, :cut], -2), ring_shift(chunks[2, cut:], 2)]
+    return [chunks[0], ring_shift(chunks[1], -1), far, ring_shift(chunks[3], 1)]
+
+
+def joined(pieces, shape, axis):
+    pieces = [jnp.concatenate(piece) if isinstance(piece, list) else piece for piece in pieces]
+    return jnp.stack([piece.reshape(shape) for piece in pieces], axis=axis)
 
 
 def pick(flag, first, second):
@@ -96,10 +101,9 @@
     first = outgoing[:half_rows].reshape(n_plane, half_rows // n_plane, wide)
     second = outgoing[half_rows:].reshape(n_z, half_rows // n_z, wide)
     first = plane_a2a(first)
-    second = ring_out(second)
+    second = joined(ring_out(second), (n_plane, capacity, wide), 1)
     first = first.reshape(n_plane, n_z, capacity, wide).transpose(1, 0, 2, 3)
-    second = second.reshape(n_z, n_plane, capacity, wide).transpose(1, 0, 2, 3)
-    first = ring_out(first.reshape(n_z, half_rows // n_z, wide))
+    first = joined(ring_out(first.reshape(n_z, half_rows // n_z, wide)), (half_rows // n_z, wide), 0)
     second = plane_a2a(second.reshape(n_plane, half_rows // n_plane, wide))
     arrived = [first.reshape(half_rows, wide), second.reshape(half_rows, wide)]
 
@@ -119,12 +123,11 @@
     keep, send = pick(core == 0, part_even, part_odd)
     paired = (keep.astype(jnp.float32) + pair_swap(send, "core").astype(jnp.float32)).astype(jnp.bfloat16)
 
-    first = ring_back(paired[0].reshape(n_z, half_rows // n_z, wide))
+    first = joined(ring_back(paired[0].reshape(n_z, half_rows // n_z, wide)), (n_plane, capacity, wide), 1)
     second = plane_a2a(paired[1].reshape(n_plane, half_rows // n_plane, wide))
-    first = first.reshape(n_z, n_plane, capacity, wide).transpose(1, 0, 2, 3)
     second = second.reshape(n_plane, n_z, capacity, wide).transpose(1, 0, 2, 3)
     first = plane_a2a(first.reshape(n_plane, half_rows // n_plane, wide))
-    second = ring_back(second.reshape(n_z, half_rows // n_z, wide))
+    second = joined(ring_back(second.reshape(n_z, half_rows // n_z, wide)), (half_rows // n_z, wide), 0)
     returned = jnp.concatenate([first.reshape(half_rows, wide), second.reshape(half_rows, wide)])
     weighted = jnp.dot(
         mixing,

time: 183 us -> 183 us (level)
    another operation x4 -> x6, other arithmetic: 4.47 us -> 5.43 us  [joined(): return jnp.stack([piece.reshape(shape) for piece in pieces], axis=axis)]
where the time goes in v1:
time: 183 us; the launch traced here: 182 us
  starting transfers between devices  69.9 us (38%)
  waiting for transfers between devices  57.4 us (31%)
  local copies, waits for them, and re-layouts  29.2 us (16%)
  other arithmetic  16.6 us (9%)
  matrix products  8.63 us (5%)
    ppermute x16, waiting for transfers between devices, ring_shift(): lax.ppermute(value, RING, [(i, (i + shift) % size) for i in range(size)])  39.7 us
    ppermute x16, starting transfers between devices, ring_shift(): lax.ppermute(value, RING, [(i, (i + shift) % size) for i in range(size)])  30.2 us
    all_to_all x4, starting transfers between devices, plane_a2a(): return lax.all_to_all(value, PLANE, 0, 0, tiled=True)  29.2 us
    ppermute x4, waiting for transfers between devices, pair_swap(): return lax.ppermute(value, axis, [(0, 1), (1, 0)])  17.6 us
    ppermute x4, starting transfers between devices, pair_swap(): return lax.ppermute(value, axis, [(0, 1), (1, 0)])  10.5 us
    another operation x6, other arithmetic, joined(): return jnp.stack([piece.reshape(shape) for piece in pieces], axis=axis)  5.43 us
    unnamed x18, local copies, waits for them, and re-layouts  5.21 us
    select_n x3, other arithmetic, pick(): return (jnp.where(flag, first, second), jnp.where(flag, second, first))  3.73 us
  transfers between devices with their start and end apart: 24, of which 18 were waited for; matrix products, arithmetic and copies ran while one was open for 18% of the time, Pallas kernels for 0%

profile of v1, /device:TPU:2, one launch (start us, length us, event | category | flops | bytes accessed | tf_op | source)
XLA Modules:
  0.0 182.1 jit_solution(6653626261366316798)
XLA Ops:
  0.0 7.2 %collective-permute-start = (bf16[64,896]{1,0:T(8,128)(2,1)}, bf16[64,896]{1,0:T(8,128)(2,1)S(1)}, u32[]{:S(2)}, u32[]{:S(2)}) collective-permute-start(bf16[64,896]{1,0:T(8,128)(2,1)} %param.6), channel_id=1, source_target_pairs={{0,128},{128,0},{1,129},{129,1},{2,130},{130,2},{3,131},{131,3},{4... | collective-permute-start | bytes 344072 | tf_op jit(solution)/shard_map/ppermute | solution.py:15
  13.1 1.7 fusion.64
  14.8 7.5 %all-to-all-start = ((bf16[16,24,1792]{2,1,0:T(8,128)(2,1)}), bf16[16,24,1792]{2,1,0:T(8,128)(2,1)}, u32[]{:S(2)}, u32[]{:S(2)}) async-start(bf16[16,24,1792]{2,1,0:T(8,128)(2,1)} %bitcast.112), calls=%async_computation | async-start | bytes 2752512 | tf_op jit(solution)/shard_map/all_to_all | solution.py:24
  22.3 1.8 slice_bitcast_fusion.7
  24.1 3.6 %collective-permute-start.6 = (bf16[48,1792]{1,0:T(8,128)(2,1)}, bf16[48,1792]{1,0:T(8,128)(2,1)}, u32[]{:S(2)}, u32[]{:S(2)}) collective-permute-start(bf16[48,1792]{1,0:T(8,128)(2,1)} %get-tuple-element.37), channel_id=1, source_target_pairs={{0,32},{16,48},{32,128},{48,144},{128,160},{144,176},{160,0},{176,... | collective-permute-start | bytes 516104 | tf_op jit(solution)/shard_map/ppermute | solution.py:20
  27.7 2.8 %collective-permute-start.7 = (bf16[48,1792]{1,0:T(8,128)(2,1)}, bf16[48,1792]{1,0:T(8,128)(2,1)}, u32[]{:S(2)}, u32[]{:S(2)}) collective-permute-start(bf16[48,1792]{1,0:T(8,128)(2,1)} %get-tuple-element.38), channel_id=1, source_target_pairs={{0,160},{16,176},{32,0},{48,16},{128,32},{144,48},{160,128},{176,1... | collective-permute-start | bytes 516104 | tf_op jit(solution)/shard_map/ppermute | solution.py:20
  31.8 2.7 %collective-permute-start.8 = (bf16[96,1792]{1,0:T(8,128)(2,1)S(1)}, bf16[96,1792]{1,0:T(8,128)(2,1)S(1)}, u32[]{:S(2)}, u32[]{:S(2)}) collective-permute-start(bf16[96,1792]{1,0:T(8,128)(2,1)S(1)} %get-tuple-element.23), channel_id=1, source_target_pairs={{0,176},{16,0},{32,16},{48,32},{128,48},{144,128},{160,144},{176,1... | collective-permute-start | bytes 1032200 | tf_op jit(solution)/shard_map/ppermute | solution.py:20
  34.7 3.8 %collective-permute-done.6 = bf16[48,1792]{1,0:T(8,128)(2,1)} collective-permute-done((bf16[48,1792]{1,0:T(8,128)(2,1)}, bf16[48,1792]{1,0:T(8,128)(2,1)}, u32[]{:S(2)}, u32[]{:S(2)}) %collective-permute-start.6) | collective-permute-done | bytes 172064 | tf_op jit(solution)/shard_map/ppermute | solution.py:20
  39.6 4.3 %collective-permute-done.5 = bf16[96,1792]{1,0:T(8,128)(2,1)S(1)} collective-permute-done((bf16[96,1792]{1,0:T(8,128)(2,1)}, bf16[96,1792]{1,0:T(8,128)(2,1)S(1)}, u32[]{:S(2)}, u32[]{:S(2)}) %collective-permute-start.5) | collective-permute-done | bytes 344096 | tf_op jit(solution)/shard_map/ppermute | solution.py:20
  45.8 1.5 copy.86
  47.3 7.2 %all-to-all-start.1 = ((bf16[16,24,1792]{2,1,0:T(8,128)(2,1)}), bf16[16,24,1792]{2,1,0:T(8,128)(2,1)S(1)}, u32[]{:S(2)}, u32[]{:S(2)}) async-start(bf16[16,24,1792]{2,1,0:T(8,128)(2,1)} %copy.86), calls=%async_computation.1 | async-start | bytes 2752512 | tf_op jit(solution)/shard_map/all_to_all | solution.py:24
  54.6 1.6 copy.78
  60.4 3.0 %collective-permute-start.3 = (bf16[48,1792]{1,0:T(8,128)(2,1)}, bf16[48,1792]{1,0:T(8,128)(2,1)}, u32[]{:S(2)}, u32[]{:S(2)}) collective-permute-start(bf16[48,1792]{1,0:T(8,128)(2,1)} %bitcast.101), channel_id=1, source_target_pairs={{0,160},{16,176},{32,0},{48,16},{128,32},{144,48},{160,128},{176,1... | collective-permute-start | bytes 516104 | tf_op jit(solution)/shard_map/ppermute | solution.py:20
  64.2 3.2 %collective-permute-start.4 = (bf16[96,1792]{1,0:T(8,128)(2,1)S(1)}, bf16[96,1792]{1,0:T(8,128)(2,1)}, u32[]{:S(2)}, u32[]{:S(2)}) collective-permute-start(bf16[96,1792]{1,0:T(8,128)(2,1)S(1)} %squeeze.62), channel_id=1, source_target_pairs={{0,176},{16,0},{32,16},{48,32},{128,48},{144,128},{160,144},{176,1... | collective-permute-start | bytes 1032200 | tf_op jit(solution)/shard_map/ppermute | solution.py:20
  67.6 3.8 %collective-permute-done.2 = bf16[48,1792]{1,0:T(8,128)(2,1)S(1)} collective-permute-done((bf16[48,1792]{1,0:T(8,128)(2,1)}, bf16[48,1792]{1,0:T(8,128)(2,1)S(1)}, u32[]{:S(2)}, u32[]{:S(2)}) %collective-permute-start.2) | collective-permute-done | bytes 172064 | tf_op jit(solution)/shard_map/ppermute | solution.py:20
  73.2 2.0 %collective-permute-done.1 = bf16[96,1792]{1,0:T(8,128)(2,1)} collective-permute-done((bf16[96,1792]{1,0:T(8,128)(2,1)S(1)}, bf16[96,1792]{1,0:T(8,128)(2,1)}, u32[]{:S(2)}, u32[]{:S(2)}) %collective-permute-start.1) | collective-permute-done | bytes 344096 | tf_op jit(solution)/shard_map/ppermute | solution.py:20
  75.2 1.5 collective-permute-done.4
  76.7 1.3 pad_maximum_fusion.5
  78.0 1.8 pad_maximum_fusion
  79.7 5.4 %collective-permute-done.9 = bf16[2,384,1792]{2,1,0:T(8,128)(2,1)} collective-permute-done((bf16[2,384,1792]{2,1,0:T(8,128)(2,1)}, bf16[2,384,1792]{2,1,0:T(8,128)(2,1)}, u32[]{:S(2)}, u32[]{:S(2)}) %collective-permute-start.9) | collective-permute-done | bytes 2752544 | tf_op jit(solution)/shard_map/ppermute | solution.py:15
  85.2 2.1 %broadcast_select_fusion.2 = (bf16[2,384,1792]{2,1,0:T(8,128)(2,1)S(1)}, bf16[2,384,1792]{2,1,0:T(8,128)(2,1)S(1)}) fusion(bf16[2,384,1792]{2,1,0:T(8,128)(2,1)} %collective-permute-done.9, pred[]{:T(512)S(6)} %eq.95, bf16[1,384,1792]{2,1,0:T(8,128)(2,1)S(1)} %bitcast.104, bf16[1,384,1792]{2,1,0:T(8,128)(2,1)S(1)} %bitcast.106), kind=kLoop, calls=%fused_computation.21 | loop fusion | flops 4128768 | bytes 11010049 | tf_op jit(solution)/shard_map/jit(_where)/select_n | solution.py:45
  88.2 1.2 slice-done.1
  89.4 3.3 %fusion = f32[2,384,2,256]{3,1,2,0:T(8,128)S(1)} fusion(bf16[2,3584,2,256]{3,2,1,0:T(2,128)(2,1)S(1)} %bitcast.125, bf16[2,384,896]{2,1,0:T(8,128)(2,1)S(1)} %get-tuple-element.43, bf16[2,384,896]{2,1,0:T(8,128)(2,1)S(1)} %get-tuple-element.17, bf16[2,384,896]{2,1,0:T(8,128)(2,1)S(1)} %get-tuple-element.44, bf16[2,384,896]{2,1,0:T(8,128)(2,1)S(1)} %get-tuple-element.16), kind=kOutput, calls=%fused_computation | convolution fusion | flops 2840592384 | bytes 14417920 | tf_op jit(solution)/shard_map/srd,sdgf->srgf/dot_general | solution.py:116
  92.7 1.6 convolution_convert_fusion
  96.0 5.0 %collective-permute-done.10 = bf16[2,384,1792]{2,1,0:T(8,128)(2,1)S(1)} collective-permute-done((bf16[2,384,1792]{2,1,0:T(8,128)(2,1)S(1)}, bf16[2,384,1792]{2,1,0:T(8,128)(2,1)S(1)}, u32[]{:S(2)}, u32[]{:S(2)}) %collective-permute-start.10) | collective-permute-done | bytes 2752544 | tf_op jit(solution)/shard_map/ppermute | solution.py:15
  101.0 1.1 add_convert_fusion
  102.1 1.7 fusion.61
  103.9 7.2 %all-to-all-start.3 = ((bf16[16,24,1792]{2,1,0:T(8,128)(2,1)}), bf16[16,24,1792]{2,1,0:T(8,128)(2,1)}, u32[]{:S(2)}, u32[]{:S(2)}) async-start(bf16[16,24,1792]{2,1,0:T(8,128)(2,1)} %bitcast.111), calls=%async_computation.3 | async-start | bytes 2752512 | tf_op jit(solution)/shard_map/all_to_all | solution.py:24
  111.1 1.8 slice_bitcast_fusion.5
  112.9 3.2 %collective-permute-start.12 = (bf16[48,1792]{1,0:T(8,128)(2,1)}, bf16[48,1792]{1,0:T(8,128)(2,1)}, u32[]{:S(2)}, u32[]{:S(2)}) collective-permute-start(bf16[48,1792]{1,0:T(8,128)(2,1)} %get-tuple-element.25), channel_id=1, source_target_pairs={{0,160},{16,176},{32,0},{48,16},{128,32},{144,48},{160,128},{176,1... | collective-permute-start | bytes 516104 | tf_op jit(solution)/shard_map/ppermute | solution.py:20
  116.9 4.7 %collective-permute-start.11 = (bf16[96,1792]{1,0:T(8,128)(2,1)}, bf16[96,1792]{1,0:T(8,128)(2,1)S(1)}, u32[]{:S(2)}, u32[]{:S(2)}) collective-permute-start(bf16[96,1792]{1,0:T(8,128)(2,1)} %get-tuple-element.13), channel_id=1, source_target_pairs={{0,176},{16,0},{32,16},{48,32},{128,48},{144,128},{160,144},{176,1... | collective-permute-start | bytes 1032200 | tf_op jit(solution)/shard_map/ppermute | solution.py:20
  121.9 2.7 %collective-permute-done.12 = bf16[48,1792]{1,0:T(8,128)(2,1)} collective-permute-done((bf16[48,1792]{1,0:T(8,128)(2,1)}, bf16[48,1792]{1,0:T(8,128)(2,1)}, u32[]{:S(2)}, u32[]{:S(2)}) %collective-permute-start.12) | collective-permute-done | bytes 172064 | tf_op jit(solution)/shard_map/ppermute | solution.py:20
  124.6 4.3 %collective-permute-done.13 = bf16[48,1792]{1,0:T(8,128)(2,1)} collective-permute-done((bf16[48,1792]{1,0:T(8,128)(2,1)}, bf16[48,1792]{1,0:T(8,128)(2,1)}, u32[]{:S(2)}, u32[]{:S(2)}) %collective-permute-start.13) | collective-permute-done | bytes 172064 | tf_op jit(solution)/shard_map/ppermute | solution.py:20
  130.0 1.9 %collective-permute-done.11 = bf16[96,1792]{1,0:T(8,128)(2,1)S(1)} collective-permute-done((bf16[96,1792]{1,0:T(8,128)(2,1)}, bf16[96,1792]{1,0:T(8,128)(2,1)S(1)}, u32[]{:S(2)}, u32[]{:S(2)}) %collective-permute-start.11) | collective-permute-done | bytes 344096 | tf_op jit(solution)/shard_map/ppermute | solution.py:20
  132.0 3.4 %collective-permute-done.14 = bf16[96,1792]{1,0:T(8,128)(2,1)S(1)} collective-permute-done((bf16[96,1792]{1,0:T(8,128)(2,1)S(1)}, bf16[96,1792]{1,0:T(8,128)(2,1)S(1)}, u32[]{:S(2)}, u32[]{:S(2)}) %collective-permute-start.14) | collective-permute-done | bytes 344096 | tf_op jit(solution)/shard_map/ppermute | solution.py:20
  136.2 1.5 copy.90
  137.8 7.2 %all-to-all-start.2 = ((bf16[16,24,1792]{2,1,0:T(8,128)(2,1)}), bf16[16,24,1792]{2,1,0:T(8,128)(2,1)S(1)}, u32[]{:S(2)}, u32[]{:S(2)}) async-start(bf16[16,24,1792]{2,1,0:T(8,128)(2,1)} %copy.90), calls=%async_computation.2 | async-start | bytes 2752512 | tf_op jit(solution)/shard_map/all_to_all | solution.py:24
  145.0 1.6 copy.91
  149.8 2.9 %collective-permute-start.17 = (bf16[48,1792]{1,0:T(8,128)(2,1)}, bf16[48,1792]{1,0:T(8,128)(2,1)}, u32[]{:S(2)}, u32[]{:S(2)}) collective-permute-start(bf16[48,1792]{1,0:T(8,128)(2,1)} %bitcast.99), channel_id=1, source_target_pairs={{0,32},{16,48},{32,128},{48,144},{128,160},{144,176},{160,0},{176,... | collective-permute-start | bytes 516104 | tf_op jit(solution)/shard_map/ppermute | solution.py:20
  153.0 1.2 collective-permute-start.15
  155.4 1.2 select_reduce_fusion
  158.0 2.9 %collective-permute-done.17 = bf16[48,1792]{1,0:T(8,128)(2,1)} collective-permute-done((bf16[48,1792]{1,0:T(8,128)(2,1)}, bf16[48,1792]{1,0:T(8,128)(2,1)}, u32[]{:S(2)}, u32[]{:S(2)}) %collective-permute-start.17) | collective-permute-done | bytes 172064 | tf_op jit(solution)/shard_map/ppermute | solution.py:20
  161.9 3.2 %collective-permute-done.15 = bf16[96,1792]{1,0:T(8,128)(2,1)S(1)} collective-permute-done((bf16[96,1792]{1,0:T(8,128)(2,1)S(1)}, bf16[96,1792]{1,0:T(8,128)(2,1)S(1)}, u32[]{:S(2)}, u32[]{:S(2)}) %collective-permute-start.15) | collective-permute-done | bytes 344096 | tf_op jit(solution)/shard_map/ppermute | solution.py:20
  165.1 3.1 %collective-permute-done.18 = bf16[96,1792]{1,0:T(8,128)(2,1)} collective-permute-done((bf16[96,1792]{1,0:T(8,128)(2,1)S(1)}, bf16[96,1792]{1,0:T(8,128)(2,1)}, u32[]{:S(2)}, u32[]{:S(2)}) %collective-permute-start.18) | collective-permute-done | bytes 344096 | tf_op jit(solution)/shard_map/ppermute | solution.py:20
  168.3 1.3 pad_maximum_fusion.6
  169.6 1.5 fusion.8
  171.1 3.1 %collective-permute-start.19 = (bf16[64,896]{1,0:T(8,128)(2,1)S(1)}, bf16[64,896]{1,0:T(8,128)(2,1)S(1)}, u32[]{:S(2)}, u32[]{:S(2)}) collective-permute-start(bf16[64,896]{1,0:T(8,128)(2,1)S(1)} %select_convert_fusion), channel_id=1, source_target_pairs={{0,128},{128,0},{1,129},{129,1},{2,130},{130,2},{3,131},{131,3},{4... | collective-permute-start | bytes 344072 | tf_op jit(solution)/shard_map/ppermute | solution.py:15
  174.2 7.2 %collective-permute-done.19 = bf16[64,896]{1,0:T(8,128)(2,1)S(1)} collective-permute-done((bf16[64,896]{1,0:T(8,128)(2,1)S(1)}, bf16[64,896]{1,0:T(8,128)(2,1)S(1)}, u32[]{:S(2)}, u32[]{:S(2)}) %collective-permute-start.19) | collective-permute-done | bytes 114720 | tf_op jit(solution)/shard_map/ppermute | solution.py:15
  (91 shorter events, 30.8 us)
Async XLA Ops:
  0.0 11.3 %collective-permute-start = (bf16[64,896]{1,0:T(8,128)(2,1)}, bf16[64,896]{1,0:T(8,128)(2,1)S(1)}, u32[]{:S(2)}, u32[]{:S(2)}) collective-permute-start(bf16[64,896]{1,0:T(8,128)(2,1)} %param.6), channel_id=1, source_target_pairs={{0,128},{128,0},{1,129},{129,1},{2,130},{130,2},{3,131},{131,3},{4... | collective-permute-start | bytes 344072 | tf_op jit(solution)/shard_map/ppermute | solution.py:15
  14.8 32.5 %all-to-all-start = ((bf16[16,24,1792]{2,1,0:T(8,128)(2,1)}), bf16[16,24,1792]{2,1,0:T(8,128)(2,1)}, u32[]{:S(2)}, u32[]{:S(2)}) async-start(bf16[16,24,1792]{2,1,0:T(8,128)(2,1)} %bitcast.112), calls=%async_computation | async-start | bytes 2752512 | tf_op jit(solution)/shard_map/all_to_all | solution.py:24
  24.1 14.3 %collective-permute-start.6 = (bf16[48,1792]{1,0:T(8,128)(2,1)}, bf16[48,1792]{1,0:T(8,128)(2,1)}, u32[]{:S(2)}, u32[]{:S(2)}) collective-permute-start(bf16[48,1792]{1,0:T(8,128)(2,1)} %get-tuple-element.37), channel_id=1, source_target_pairs={{0,32},{16,48},{32,128},{48,144},{128,160},{144,176},{160,0},{176,... | collective-permute-start | bytes 516104 | tf_op jit(solution)/shard_map/ppermute | solution.py:20
  27.7 10.7 %collective-permute-start.7 = (bf16[48,1792]{1,0:T(8,128)(2,1)}, bf16[48,1792]{1,0:T(8,128)(2,1)}, u32[]{:S(2)}, u32[]{:S(2)}) collective-permute-start(bf16[48,1792]{1,0:T(8,128)(2,1)} %get-tuple-element.38), channel_id=1, source_target_pairs={{0,160},{16,176},{32,0},{48,16},{128,32},{144,48},{160,128},{176,1... | collective-permute-start | bytes 516104 | tf_op jit(solution)/shard_map/ppermute | solution.py:20
  31.3 12.5 %collective-permute-start.5 = (bf16[96,1792]{1,0:T(8,128)(2,1)}, bf16[96,1792]{1,0:T(8,128)(2,1)S(1)}, u32[]{:S(2)}, u32[]{:S(2)}) collective-permute-start(bf16[96,1792]{1,0:T(8,128)(2,1)} %get-tuple-element.24), channel_id=1, source_target_pairs={{0,16},{16,32},{32,48},{48,128},{128,144},{144,160},{160,176},{176... | collective-permute-start | bytes 1032200 | tf_op jit(solution)/shard_map/ppermute | solution.py:20
  31.8 13.2 %collective-permute-start.8 = (bf16[96,1792]{1,0:T(8,128)(2,1)S(1)}, bf16[96,1792]{1,0:T(8,128)(2,1)S(1)}, u32[]{:S(2)}, u32[]{:S(2)}) collective-permute-start(bf16[96,1792]{1,0:T(8,128)(2,1)S(1)} %get-tuple-element.23), channel_id=1, source_target_pairs={{0,176},{16,0},{32,16},{48,32},{128,48},{144,128},{160,144},{176,1... | collective-permute-start | bytes 1032200 | tf_op jit(solution)/shard_map/ppermute | solution.py:20
  47.3 30.6 %all-to-all-start.1 = ((bf16[16,24,1792]{2,1,0:T(8,128)(2,1)}), bf16[16,24,1792]{2,1,0:T(8,128)(2,1)S(1)}, u32[]{:S(2)}, u32[]{:S(2)}) async-start(bf16[16,24,1792]{2,1,0:T(8,128)(2,1)} %copy.86), calls=%async_computation.1 | async-start | bytes 2752512 | tf_op jit(solution)/shard_map/all_to_all | solution.py:24
  58.6 12.8 %collective-permute-start.2 = (bf16[48,1792]{1,0:T(8,128)(2,1)}, bf16[48,1792]{1,0:T(8,128)(2,1)S(1)}, u32[]{:S(2)}, u32[]{:S(2)}) collective-permute-start(bf16[48,1792]{1,0:T(8,128)(2,1)} %bitcast.102), channel_id=1, source_target_pairs={{0,32},{16,48},{32,128},{48,144},{128,160},{144,176},{160,0},{176,... | collective-permute-start | bytes 516104 | tf_op jit(solution)/shard_map/ppermute | solution.py:20
  60.4 11.9 %collective-permute-start.3 = (bf16[48,1792]{1,0:T(8,128)(2,1)}, bf16[48,1792]{1,0:T(8,128)(2,1)}, u32[]{:S(2)}, u32[]{:S(2)}) collective-permute-start(bf16[48,1792]{1,0:T(8,128)(2,1)} %bitcast.101), channel_id=1, source_target_pairs={{0,160},{16,176},{32,0},{48,16},{128,32},{144,48},{160,128},{176,1... | collective-permute-start | bytes 516104 | tf_op jit(solution)/shard_map/ppermute | solution.py:20
  63.8 11.4 %collective-permute-start.1 = (bf16[96,1792]{1,0:T(8,128)(2,1)S(1)}, bf16[96,1792]{1,0:T(8,128)(2,1)}, u32[]{:S(2)}, u32[]{:S(2)}) collective-permute-start(bf16[96,1792]{1,0:T(8,128)(2,1)S(1)} %squeeze.59), channel_id=1, source_target_pairs={{0,16},{16,32},{32,48},{48,128},{128,144},{144,160},{160,176},{176... | collective-permute-start | bytes 1032200 | tf_op jit(solution)/shard_map/ppermute | solution.py:20
  64.2 12.5 %collective-permute-start.4 = (bf16[96,1792]{1,0:T(8,128)(2,1)S(1)}, bf16[96,1792]{1,0:T(8,128)(2,1)}, u32[]{:S(2)}, u32[]{:S(2)}) collective-permute-start(bf16[96,1792]{1,0:T(8,128)(2,1)S(1)} %squeeze.62), channel_id=1, source_target_pairs={{0,176},{16,0},{32,16},{48,32},{128,48},{144,128},{160,144},{176,1... | collective-permute-start | bytes 1032200 | tf_op jit(solution)/shard_map/ppermute | solution.py:20
  79.7 5.4 %collective-permute-start.9 = (bf16[2,384,1792]{2,1,0:T(8,128)(2,1)}, bf16[2,384,1792]{2,1,0:T(8,128)(2,1)}, u32[]{:S(2)}, u32[]{:S(2)}) collective-permute-start(bf16[2,384,1792]{2,1,0:T(8,128)(2,1)} %pad_maximum_fusion), channel_id=1, source_target_pairs={{0,64},{64,0},{1,65},{65,1},{2,66},{66,2},{3,67},{67,3},{4,68},{68... | collective-permute-start | bytes 8257544 | tf_op jit(solution)/shard_map/ppermute | solution.py:15
  85.2 3.0 %slice-start = ((s8[7340032]{0:T(1024)(128)(4,1)}), s8[4194304]{0:T(1024)(128)(4,1)S(1)}, s32[]{:S(2)}) async-start(s8[7340032]{0:T(1024)(128)(4,1)} %bitcast.124), calls=%async_computation.4 | async-start | bytes 8388608
  87.3 2.1 %slice-start.1 = ((s8[7340032]{0:T(1024)(128)(4,1)}), s8[3145728]{0:T(1024)(128)(4,1)S(1)}, s32[]{:S(2)}) async-start(s8[7340032]{0:T(1024)(128)(4,1)} %bitcast.124), calls=%async_computation.5 | async-start | bytes 6291456
  89.4 3.3 %copy-start = (bf16[2,256,3584]{2,1,0:T(8,128)(2,1)S(1)}, bf16[2,256,3584]{2,1,0:T(8,128)(2,1)}, u32[]{:S(2)}) copy-start(bf16[2,256,3584]{2,1,0:T(8,128)(2,1)} %param.11) | copy-start | bytes 11010052
  95.8 5.2 %collective-permute-start.10 = (bf16[2,384,1792]{2,1,0:T(8,128)(2,1)S(1)}, bf16[2,384,1792]{2,1,0:T(8,128)(2,1)S(1)}, u32[]{:S(2)}, u32[]{:S(2)}) collective-permute-start(bf16[2,384,1792]{2,1,0:T(8,128)(2,1)S(1)} %broadcast_select_fusion), channel_id=1, source_target_pairs={{0,64},{64,0},{1,65},{65,1},{2,66},{66,2},{3,67},{67,3},{4,68},{68... | collective-permute-start | bytes 8257544 | tf_op jit(solution)/shard_map/ppermute | solution.py:15
  103.9 33.9 %all-to-all-start.3 = ((bf16[16,24,1792]{2,1,0:T(8,128)(2,1)}), bf16[16,24,1792]{2,1,0:T(8,128)(2,1)}, u32[]{:S(2)}, u32[]{:S(2)}) async-start(bf16[16,24,1792]{2,1,0:T(8,128)(2,1)} %bitcast.111), calls=%async_computation.3 | async-start | bytes 2752512 | tf_op jit(solution)/shard_map/all_to_all | solution.py:24
  111.1 10.6 %copy-start.3 = (f32[64,8]{0,1:T(8,128)S(1)}, f32[64,8]{0,1:T(8,128)}, u32[]{:S(2)}) copy-start(f32[64,8]{0,1:T(8,128)} %param.8) | copy-start | bytes 6148
  112.9 11.7 %collective-permute-start.12 = (bf16[48,1792]{1,0:T(8,128)(2,1)}, bf16[48,1792]{1,0:T(8,128)(2,1)}, u32[]{:S(2)}, u32[]{:S(2)}) collective-permute-start(bf16[48,1792]{1,0:T(8,128)(2,1)} %get-tuple-element.25), channel_id=1, source_target_pairs={{0,160},{16,176},{32,0},{48,16},{128,32},{144,48},{160,128},{176,1... | collective-permute-start | bytes 516104 | tf_op jit(solution)/shard_map/ppermute | solution.py:20
  116.1 12.7 %collective-permute-start.13 = (bf16[48,1792]{1,0:T(8,128)(2,1)}, bf16[48,1792]{1,0:T(8,128)(2,1)}, u32[]{:S(2)}, u32[]{:S(2)}) collective-permute-start(bf16[48,1792]{1,0:T(8,128)(2,1)} %get-tuple-element.26), channel_id=1, source_target_pairs={{0,32},{16,48},{32,128},{48,144},{128,160},{144,176},{160,0},{176,... | collective-permute-start | bytes 516104 | tf_op jit(solution)/shard_map/ppermute | solution.py:20
  116.9 15.0 %collective-permute-start.11 = (bf16[96,1792]{1,0:T(8,128)(2,1)}, bf16[96,1792]{1,0:T(8,128)(2,1)S(1)}, u32[]{:S(2)}, u32[]{:S(2)}) collective-permute-start(bf16[96,1792]{1,0:T(8,128)(2,1)} %get-tuple-element.13), channel_id=1, source_target_pairs={{0,176},{16,0},{32,16},{48,32},{128,48},{144,128},{160,144},{176,1... | collective-permute-start | bytes 1032200 | tf_op jit(solution)/shard_map/ppermute | solution.py:20
  121.6 13.8 %collective-permute-start.14 = (bf16[96,1792]{1,0:T(8,128)(2,1)S(1)}, bf16[96,1792]{1,0:T(8,128)(2,1)S(1)}, u32[]{:S(2)}, u32[]{:S(2)}) collective-permute-start(bf16[96,1792]{1,0:T(8,128)(2,1)S(1)} %get-tuple-element.12), channel_id=1, source_target_pairs={{0,16},{16,32},{32,48},{48,128},{128,144},{144,160},{160,176},{176... | collective-permute-start | bytes 1032200 | tf_op jit(solution)/shard_map/ppermute | solution.py:20
  137.8 31.7 %all-to-all-start.2 = ((bf16[16,24,1792]{2,1,0:T(8,128)(2,1)}), bf16[16,24,1792]{2,1,0:T(8,128)(2,1)S(1)}, u32[]{:S(2)}, u32[]{:S(2)}) async-start(bf16[16,24,1792]{2,1,0:T(8,128)(2,1)} %copy.90), calls=%async_computation.2 | async-start | bytes 2752512 | tf_op jit(solution)/shard_map/all_to_all | solution.py:24
  149.1 8.9 %collective-permute-start.16 = (bf16[48,1792]{1,0:T(8,128)(2,1)}, bf16[48,1792]{1,0:T(8,128)(2,1)}, u32[]{:S(2)}, u32[]{:S(2)}) collective-permute-start(bf16[48,1792]{1,0:T(8,128)(2,1)} %bitcast.100), channel_id=1, source_target_pairs={{0,160},{16,176},{32,0},{48,16},{128,32},{144,48},{160,128},{176,1... | collective-permute-start | bytes 516104 | tf_op jit(solution)/shard_map/ppermute | solution.py:20
  149.8 11.1 %collective-permute-start.17 = (bf16[48,1792]{1,0:T(8,128)(2,1)}, bf16[48,1792]{1,0:T(8,128)(2,1)}, u32[]{:S(2)}, u32[]{:S(2)}) collective-permute-start(bf16[48,1792]{1,0:T(8,128)(2,1)} %bitcast.99), channel_id=1, source_target_pairs={{0,32},{16,48},{32,128},{48,144},{128,160},{144,176},{160,0},{176,... | collective-permute-start | bytes 516104 | tf_op jit(solution)/shard_map/ppermute | solution.py:20
  153.0 12.1 %collective-permute-start.15 = (bf16[96,1792]{1,0:T(8,128)(2,1)S(1)}, bf16[96,1792]{1,0:T(8,128)(2,1)S(1)}, u32[]{:S(2)}, u32[]{:S(2)}) collective-permute-start(bf16[96,1792]{1,0:T(8,128)(2,1)S(1)} %squeeze.71), channel_id=1, source_target_pairs={{0,176},{16,0},{32,16},{48,32},{128,48},{144,128},{160,144},{176,1... | collective-permute-start | bytes 1032200 | tf_op jit(solution)/shard_map/ppermute | solution.py:20
  154.4 13.9 %collective-permute-start.18 = (bf16[96,1792]{1,0:T(8,128)(2,1)S(1)}, bf16[96,1792]{1,0:T(8,128)(2,1)}, u32[]{:S(2)}, u32[]{:S(2)}) collective-permute-start(bf16[96,1792]{1,0:T(8,128)(2,1)S(1)} %squeeze.74), channel_id=1, source_target_pairs={{0,16},{16,32},{32,48},{48,128},{128,144},{144,160},{160,176},{176... | collective-permute-start | bytes 1032200 | tf_op jit(solution)/shard_map/ppermute | solution.py:20
  156.9 12.7 %copy-start.2 = (f32[64,768]{1,0:T(8,128)S(1)}, f32[64,768]{1,0:T(8,128)}, u32[]{:S(2)}) copy-start(f32[64,768]{1,0:T(8,128)} %select_reduce_fusion) | copy-start | bytes 589828
  165.1 3.1 %copy-start.1 = (bf16[96,1792]{1,0:T(8,128)(2,1)}, bf16[96,1792]{1,0:T(8,128)(2,1)S(1)}, u32[]{:S(2)}) copy-start(bf16[96,1792]{1,0:T(8,128)(2,1)S(1)} %collective-permute-done.15) | copy-start | bytes 1032196
  171.1 10.3 %collective-permute-start.19 = (bf16[64,896]{1,0:T(8,128)(2,1)S(1)}, bf16[64,896]{1,0:T(8,128)(2,1)S(1)}, u32[]{:S(2)}, u32[]{:S(2)}) collective-permute-start(bf16[64,896]{1,0:T(8,128)(2,1)S(1)} %select_convert_fusion), channel_id=1, source_target_pairs={{0,128},{128,0},{1,129},{129,1},{2,130},{130,2},{3,131},{131,3},{4... | collective-permute-start | bytes 344072 | tf_op jit(solution)/shard_map/ppermute | solution.py:15

commit v2 on v1

--- a/solution.py
+++ b/solution.py
@@ -89,6 +89,7 @@
     gather = jnp.sum(hits.astype(jnp.bfloat16), axis=1)
     mixing = jnp.sum(jnp.where(hits, route_weights[:, :, None], 0.0), axis=1)
 
+    gather, mixing, tokens = lax.optimization_barrier((gather, mixing, tokens))
     other = pair_swap(tokens, "zh")
     low, high = pick(half == 0, tokens, other)
     features = jnp.concatenate([low, high], axis=1)

time: 183 us -> 188 us (1.027)
  waiting for transfers between devices: 57.4 us -> 64.1 us
    ppermute x4, waiting for transfers between devices: 17.6 us -> 22.9 us  [pair_swap(): return lax.ppermute(value, axis, [(0, 1), (1, 0)])]
    unnamed x18 -> x16, local copies, waits for them, and re-layouts: 5.21 us -> 5.21 us
  transfers between devices with their start and end apart: 24 -> 24, of which waited for: 18 -> 17; matrix products, arithmetic and copies ran while one was open for 18% -> 15% of each run, Pallas kernels for 0% -> 0%
where the time goes in v2:
time: 188 us; the launch traced here: 187 us
  starting transfers between devices  68.4 us (36%)
  waiting for transfers between devices  64.1 us (34%)
  local copies, waits for them, and re-layouts  29.1 us (15%)
  other arithmetic  16.7 us (9%)
  matrix products  8.63 us (5%)
    ppermute x16, waiting for transfers between devices, ring_shift(): lax.ppermute(value, RING, [(i, (i + shift) % size) for i in range(size)])  41.2 us
    ppermute x16, starting transfers between devices, ring_shift(): lax.ppermute(value, RING, [(i, (i + shift) % size) for i in range(size)])  29.8 us
    all_to_all x4, starting transfers between devices, plane_a2a(): return lax.all_to_all(value, PLANE, 0, 0, tiled=True)  29.2 us
    ppermute x4, waiting for transfers between devices, pair_swap(): return lax.ppermute(value, axis, [(0, 1), (1, 0)])  22.9 us
    ppermute x4, starting transfers between devices, pair_swap(): return lax.ppermute(value, axis, [(0, 1), (1, 0)])  9.5 us
    another operation x6, other arithmetic, joined(): return jnp.stack([piece.reshape(shape) for piece in pieces], axis=axis)  5.52 us
    unnamed x16, local copies, waits for them, and re-layouts  5.21 us
  transfers between devices with their start and end apart: 24, of which 17 were waited for; matrix products, arithmetic and copies ran while one was open for 15% of the time, Pallas kernels for 0%

profile of v2, /device:TPU:2, one launch (start us, length us, event | category | flops | bytes accessed | tf_op | source)
XLA Modules:
  0.0 187.4 jit_solution(2498164283697650383)
XLA Ops:
  4.8 1.2 select_reduce_fusion
  6.1 7.2 %collective-permute-start = (bf16[64,896]{1,0:T(8,128)(2,1)}, bf16[64,896]{1,0:T(8,128)(2,1)S(1)}, u32[]{:S(2)}, u32[]{:S(2)}) collective-permute-start(bf16[64,896]{1,0:T(8,128)(2,1)} %param.6), channel_id=1, source_target_pairs={{0,128},{128,0},{1,129},{129,1},{2,130},{130,2},{3,131},{131,3},{4... | collective-permute-start | bytes 344072 | tf_op jit(solution)/shard_map/ppermute | solution.py:15
  13.2 3.5 %collective-permute-done = bf16[64,896]{1,0:T(8,128)(2,1)S(1)} collective-permute-done((bf16[64,896]{1,0:T(8,128)(2,1)}, bf16[64,896]{1,0:T(8,128)(2,1)S(1)}, u32[]{:S(2)}, u32[]{:S(2)}) %collective-permute-start) | collective-permute-done | bytes 114720 | tf_op jit(solution)/shard_map/ppermute | solution.py:15
  18.5 1.7 fusion.64
  20.2 7.5 %all-to-all-start = ((bf16[16,24,1792]{2,1,0:T(8,128)(2,1)}), bf16[16,24,1792]{2,1,0:T(8,128)(2,1)}, u32[]{:S(2)}, u32[]{:S(2)}) async-start(bf16[16,24,1792]{2,1,0:T(8,128)(2,1)} %bitcast.111), calls=%async_computation | async-start | bytes 2752512 | tf_op jit(solution)/shard_map/all_to_all | solution.py:24
  27.7 1.8 slice_bitcast_fusion.7
  29.5 4.2 %collective-permute-start.6 = (bf16[48,1792]{1,0:T(8,128)(2,1)}, bf16[48,1792]{1,0:T(8,128)(2,1)}, u32[]{:S(2)}, u32[]{:S(2)}) collective-permute-start(bf16[48,1792]{1,0:T(8,128)(2,1)} %get-tuple-element.43), channel_id=1, source_target_pairs={{0,32},{16,48},{32,128},{48,144},{128,160},{144,176},{160,0},{176,... | collective-permute-start | bytes 516104 | tf_op jit(solution)/shard_map/ppermute | solution.py:20
  33.7 2.8 %collective-permute-start.7 = (bf16[48,1792]{1,0:T(8,128)(2,1)}, bf16[48,1792]{1,0:T(8,128)(2,1)}, u32[]{:S(2)}, u32[]{:S(2)}) collective-permute-start(bf16[48,1792]{1,0:T(8,128)(2,1)} %get-tuple-element.44), channel_id=1, source_target_pairs={{0,160},{16,176},{32,0},{48,16},{128,32},{144,48},{160,128},{176,1... | collective-permute-start | bytes 516104 | tf_op jit(solution)/shard_map/ppermute | solution.py:20
  37.3 1.2 collective-permute-start.8
  39.5 4.1 %collective-permute-done.6 = bf16[48,1792]{1,0:T(8,128)(2,1)} collective-permute-done((bf16[48,1792]{1,0:T(8,128)(2,1)}, bf16[48,1792]{1,0:T(8,128)(2,1)}, u32[]{:S(2)}, u32[]{:S(2)}) %collective-permute-start.6) | collective-permute-done | bytes 172064 | tf_op jit(solution)/shard_map/ppermute | solution.py:20
  45.4 5.6 %collective-permute-done.8 = bf16[96,1792]{1,0:T(8,128)(2,1)S(1)} collective-permute-done((bf16[96,1792]{1,0:T(8,128)(2,1)}, bf16[96,1792]{1,0:T(8,128)(2,1)S(1)}, u32[]{:S(2)}, u32[]{:S(2)}) %collective-permute-start.8) | collective-permute-done | bytes 344096 | tf_op jit(solution)/shard_map/ppermute | solution.py:20
  52.0 1.5 copy.86
  53.5 7.2 %all-to-all-start.1 = ((bf16[16,24,1792]{2,1,0:T(8,128)(2,1)}), bf16[16,24,1792]{2,1,0:T(8,128)(2,1)S(1)}, u32[]{:S(2)}, u32[]{:S(2)}) async-start(bf16[16,24,1792]{2,1,0:T(8,128)(2,1)} %copy.86), calls=%async_computation.1 | async-start | bytes 2752512 | tf_op jit(solution)/shard_map/all_to_all | solution.py:24
  60.7 1.6 copy.78
  64.8 2.7 %collective-permute-start.3 = (bf16[48,1792]{1,0:T(8,128)(2,1)}, bf16[48,1792]{1,0:T(8,128)(2,1)}, u32[]{:S(2)}, u32[]{:S(2)}) collective-permute-start(bf16[48,1792]{1,0:T(8,128)(2,1)} %bitcast.101), channel_id=1, source_target_pairs={{0,160},{16,176},{32,0},{48,16},{128,32},{144,48},{160,128},{176,1... | collective-permute-start | bytes 516104 | tf_op jit(solution)/shard_map/ppermute | solution.py:20
  68.1 4.0 %collective-permute-start.4 = (bf16[96,1792]{1,0:T(8,128)(2,1)S(1)}, bf16[96,1792]{1,0:T(8,128)(2,1)}, u32[]{:S(2)}, u32[]{:S(2)}) collective-permute-start(bf16[96,1792]{1,0:T(8,128)(2,1)S(1)} %squeeze.62), channel_id=1, source_target_pairs={{0,176},{16,0},{32,16},{48,32},{128,48},{144,128},{160,144},{176,1... | collective-permute-start | bytes 1032200 | tf_op jit(solution)/shard_map/ppermute | solution.py:20
  72.7 2.3 %collective-permute-done.3 = bf16[48,1792]{1,0:T(8,128)(2,1)} collective-permute-done((bf16[48,1792]{1,0:T(8,128)(2,1)}, bf16[48,1792]{1,0:T(8,128)(2,1)}, u32[]{:S(2)}, u32[]{:S(2)}) %collective-permute-start.3) | collective-permute-done | bytes 172064 | tf_op jit(solution)/shard_map/ppermute | solution.py:20
  75.0 3.8 %collective-permute-done.2 = bf16[48,1792]{1,0:T(8,128)(2,1)} collective-permute-done((bf16[48,1792]{1,0:T(8,128)(2,1)S(1)}, bf16[48,1792]{1,0:T(8,128)(2,1)}, u32[]{:S(2)}, u32[]{:S(2)}) %collective-permute-start.2) | collective-permute-done | bytes 172064 | tf_op jit(solution)/shard_map/ppermute | solution.py:20
  79.7 2.5 %collective-permute-done.4 = bf16[96,1792]{1,0:T(8,128)(2,1)} collective-permute-done((bf16[96,1792]{1,0:T(8,128)(2,1)S(1)}, bf16[96,1792]{1,0:T(8,128)(2,1)}, u32[]{:S(2)}, u32[]{:S(2)}) %collective-permute-start.4) | collective-permute-done | bytes 344096 | tf_op jit(solution)/shard_map/ppermute | solution.py:20
  82.2 2.7 %collective-permute-done.1 = bf16[96,1792]{1,0:T(8,128)(2,1)} collective-permute-done((bf16[96,1792]{1,0:T(8,128)(2,1)S(1)}, bf16[96,1792]{1,0:T(8,128)(2,1)}, u32[]{:S(2)}, u32[]{:S(2)}) %collective-permute-start.1) | collective-permute-done | bytes 344096 | tf_op jit(solution)/shard_map/ppermute | solution.py:20
  84.9 1.3 pad_maximum_fusion.5
  86.1 1.8 pad_maximum_fusion
  87.9 5.4 %collective-permute-done.9 = bf16[2,384,1792]{2,1,0:T(8,128)(2,1)} collective-permute-done((bf16[2,384,1792]{2,1,0:T(8,128)(2,1)}, bf16[2,384,1792]{2,1,0:T(8,128)(2,1)}, u32[]{:S(2)}, u32[]{:S(2)}) %collective-permute-start.9) | collective-permute-done | bytes 2752544 | tf_op jit(solution)/shard_map/ppermute | solution.py:15
  93.4 2.1 %broadcast_select_fusion.2 = (bf16[2,384,1792]{2,1,0:T(8,128)(2,1)S(1)}, bf16[2,384,1792]{2,1,0:T(8,128)(2,1)S(1)}) fusion(bf16[2,384,1792]{2,1,0:T(8,128)(2,1)} %collective-permute-done.9, pred[]{:T(512)S(6)} %eq.95, bf16[1,384,1792]{2,1,0:T(8,128)(2,1)S(1)} %bitcast.104, bf16[1,384,1792]{2,1,0:T(8,128)(2,1)S(1)} %bitcast.106), kind=kLoop, calls=%fused_computation.21 | loop fusion | flops 4128768 | bytes 11010049 | tf_op jit(solution)/shard_map/jit(_where)/select_n | solution.py:45
  96.4 1.2 slice-done.1
  97.6 3.3 %fusion = f32[2,384,2,256]{3,1,2,0:T(8,128)S(1)} fusion(bf16[2,3584,2,256]{3,2,1,0:T(2,128)(2,1)S(1)} %bitcast.126, bf16[2,384,896]{2,1,0:T(8,128)(2,1)S(1)} %get-tuple-element.49, bf16[2,384,896]{2,1,0:T(8,128)(2,1)S(1)} %get-tuple-element.23, bf16[2,384,896]{2,1,0:T(8,128)(2,1)S(1)} %get-tuple-element.50, bf16[2,384,896]{2,1,0:T(8,128)(2,1)S(1)} %get-tuple-element.22), kind=kOutput, calls=%fused_computation | convolution fusion | flops 2840592384 | bytes 14417920 | tf_op jit(solution)/shard_map/srd,sdgf->srgf/dot_general | solution.py:117
  100.9 1.6 convolution_convert_fusion
  104.2 5.0 %collective-permute-done.10 = bf16[2,384,1792]{2,1,0:T(8,128)(2,1)S(1)} collective-permute-done((bf16[2,384,1792]{2,1,0:T(8,128)(2,1)S(1)}, bf16[2,384,1792]{2,1,0:T(8,128)(2,1)S(1)}, u32[]{:S(2)}, u32[]{:S(2)}) %collective-permute-start.10) | collective-permute-done | bytes 2752544 | tf_op jit(solution)/shard_map/ppermute | solution.py:15
  109.2 1.1 add_convert_fusion
  110.3 1.7 fusion.61
  112.0 7.2 %all-to-all-start.3 = ((bf16[16,24,1792]{2,1,0:T(8,128)(2,1)}), bf16[16,24,1792]{2,1,0:T(8,128)(2,1)}, u32[]{:S(2)}, u32[]{:S(2)}) async-start(bf16[16,24,1792]{2,1,0:T(8,128)(2,1)} %bitcast.112), calls=%async_computation.3 | async-start | bytes 2752512 | tf_op jit(solution)/shard_map/all_to_all | solution.py:24
  119.3 1.8 slice_bitcast_fusion.5
  121.0 2.9 %collective-permute-start.13 = (bf16[48,1792]{1,0:T(8,128)(2,1)}, bf16[48,1792]{1,0:T(8,128)(2,1)}, u32[]{:S(2)}, u32[]{:S(2)}) collective-permute-start(bf16[48,1792]{1,0:T(8,128)(2,1)} %get-tuple-element.32), channel_id=1, source_target_pairs={{0,32},{16,48},{32,128},{48,144},{128,160},{144,176},{160,0},{176,... | collective-permute-start | bytes 516104 | tf_op jit(solution)/shard_map/ppermute | solution.py:20
  124.8 3.2 %collective-permute-start.11 = (bf16[96,1792]{1,0:T(8,128)(2,1)S(1)}, bf16[96,1792]{1,0:T(8,128)(2,1)S(1)}, u32[]{:S(2)}, u32[]{:S(2)}) collective-permute-start(bf16[96,1792]{1,0:T(8,128)(2,1)S(1)} %get-tuple-element.19), channel_id=1, source_target_pairs={{0,176},{16,0},{32,16},{48,32},{128,48},{144,128},{160,144},{176,1... | collective-permute-start | bytes 1032200 | tf_op jit(solution)/shard_map/ppermute | solution.py:20
  128.1 2.9 %collective-permute-done.12 = bf16[48,1792]{1,0:T(8,128)(2,1)} collective-permute-done((bf16[48,1792]{1,0:T(8,128)(2,1)}, bf16[48,1792]{1,0:T(8,128)(2,1)}, u32[]{:S(2)}, u32[]{:S(2)}) %collective-permute-start.12) | collective-permute-done | bytes 172064 | tf_op jit(solution)/shard_map/ppermute | solution.py:20
  131.0 2.2 %collective-permute-done.13 = bf16[48,1792]{1,0:T(8,128)(2,1)} collective-permute-done((bf16[48,1792]{1,0:T(8,128)(2,1)}, bf16[48,1792]{1,0:T(8,128)(2,1)}, u32[]{:S(2)}, u32[]{:S(2)}) %collective-permute-start.13) | collective-permute-done | bytes 172064 | tf_op jit(solution)/shard_map/ppermute | solution.py:20
  134.4 5.9 %collective-permute-done.14 = bf16[96,1792]{1,0:T(8,128)(2,1)S(1)} collective-permute-done((bf16[96,1792]{1,0:T(8,128)(2,1)}, bf16[96,1792]{1,0:T(8,128)(2,1)S(1)}, u32[]{:S(2)}, u32[]{:S(2)}) %collective-permute-start.14) | collective-permute-done | bytes 344096 | tf_op jit(solution)/shard_map/ppermute | solution.py:20
  141.3 1.5 copy.90
  142.8 7.2 %all-to-all-start.2 = ((bf16[16,24,1792]{2,1,0:T(8,128)(2,1)}), bf16[16,24,1792]{2,1,0:T(8,128)(2,1)S(1)}, u32[]{:S(2)}, u32[]{:S(2)}) async-start(bf16[16,24,1792]{2,1,0:T(8,128)(2,1)} %copy.90), calls=%async_computation.2 | async-start | bytes 2752512 | tf_op jit(solution)/shard_map/all_to_all | solution.py:24
  150.0 1.6 copy.91
  154.8 4.1 %collective-permute-start.16 = (bf16[48,1792]{1,0:T(8,128)(2,1)}, bf16[48,1792]{1,0:T(8,128)(2,1)}, u32[]{:S(2)}, u32[]{:S(2)}) collective-permute-start(bf16[48,1792]{1,0:T(8,128)(2,1)} %bitcast.100), channel_id=1, source_target_pairs={{0,160},{16,176},{32,0},{48,16},{128,32},{144,48},{160,128},{176,1... | collective-permute-start | bytes 516104 | tf_op jit(solution)/shard_map/ppermute | solution.py:20
  160.1 2.7 %collective-permute-start.15 = (bf16[96,1792]{1,0:T(8,128)(2,1)S(1)}, bf16[96,1792]{1,0:T(8,128)(2,1)}, u32[]{:S(2)}, u32[]{:S(2)}) collective-permute-start(bf16[96,1792]{1,0:T(8,128)(2,1)S(1)} %squeeze.71), channel_id=1, source_target_pairs={{0,176},{16,0},{32,16},{48,32},{128,48},{144,128},{160,144},{176,1... | collective-permute-start | bytes 1032200 | tf_op jit(solution)/shard_map/ppermute | solution.py:20
  163.1 3.1 %collective-permute-done.17 = bf16[48,1792]{1,0:T(8,128)(2,1)} collective-permute-done((bf16[48,1792]{1,0:T(8,128)(2,1)}, bf16[48,1792]{1,0:T(8,128)(2,1)}, u32[]{:S(2)}, u32[]{:S(2)}) %collective-permute-start.17) | collective-permute-done | bytes 172064 | tf_op jit(solution)/shard_map/ppermute | solution.py:20
  167.2 4.6 %collective-permute-done.18 = bf16[96,1792]{1,0:T(8,128)(2,1)S(1)} collective-permute-done((bf16[96,1792]{1,0:T(8,128)(2,1)S(1)}, bf16[96,1792]{1,0:T(8,128)(2,1)S(1)}, u32[]{:S(2)}, u32[]{:S(2)}) %collective-permute-start.18) | collective-permute-done | bytes 344096 | tf_op jit(solution)/shard_map/ppermute | solution.py:20
  172.8 1.3 pad_maximum_fusion.6
  174.1 1.5 fusion.8
  175.6 2.1 %collective-permute-start.19 = (bf16[64,896]{1,0:T(8,128)(2,1)S(1)}, bf16[64,896]{1,0:T(8,128)(2,1)S(1)}, u32[]{:S(2)}, u32[]{:S(2)}) collective-permute-start(bf16[64,896]{1,0:T(8,128)(2,1)S(1)} %select_convert_fusion), channel_id=1, source_target_pairs={{0,128},{128,0},{1,129},{129,1},{2,130},{130,2},{3,131},{131,3},{4... | collective-permute-start | bytes 344072 | tf_op jit(solution)/shard_map/ppermute | solution.py:15
  177.7 9.0 %collective-permute-done.19 = bf16[64,896]{1,0:T(8,128)(2,1)S(1)} collective-permute-done((bf16[64,896]{1,0:T(8,128)(2,1)S(1)}, bf16[64,896]{1,0:T(8,128)(2,1)S(1)}, u32[]{:S(2)}, u32[]{:S(2)}) %collective-permute-start.19) | collective-permute-done | bytes 114720 | tf_op jit(solution)/shard_map/ppermute | solution.py:15
  (89 shorter events, 28.6 us)
Async XLA Ops:
  6.1 10.6 %collective-permute-start = (bf16[64,896]{1,0:T(8,128)(2,1)}, bf16[64,896]{1,0:T(8,128)(2,1)S(1)}, u32[]{:S(2)}, u32[]{:S(2)}) collective-permute-start(bf16[64,896]{1,0:T(8,128)(2,1)} %param.6), channel_id=1, source_target_pairs={{0,128},{128,0},{1,129},{129,1},{2,130},{130,2},{3,131},{131,3},{4... | collective-permute-start | bytes 344072 | tf_op jit(solution)/shard_map/ppermute | solution.py:15
  20.2 33.3 %all-to-all-start = ((bf16[16,24,1792]{2,1,0:T(8,128)(2,1)}), bf16[16,24,1792]{2,1,0:T(8,128)(2,1)}, u32[]{:S(2)}, u32[]{:S(2)}) async-start(bf16[16,24,1792]{2,1,0:T(8,128)(2,1)} %bitcast.111), calls=%async_computation | async-start | bytes 2752512 | tf_op jit(solution)/shard_map/all_to_all | solution.py:24
  29.5 14.1 %collective-permute-start.6 = (bf16[48,1792]{1,0:T(8,128)(2,1)}, bf16[48,1792]{1,0:T(8,128)(2,1)}, u32[]{:S(2)}, u32[]{:S(2)}) collective-permute-start(bf16[48,1792]{1,0:T(8,128)(2,1)} %get-tuple-element.43), channel_id=1, source_target_pairs={{0,32},{16,48},{32,128},{48,144},{128,160},{144,176},{160,0},{176,... | collective-permute-start | bytes 516104 | tf_op jit(solution)/shard_map/ppermute | solution.py:20
  33.7 10.5 %collective-permute-start.7 = (bf16[48,1792]{1,0:T(8,128)(2,1)}, bf16[48,1792]{1,0:T(8,128)(2,1)}, u32[]{:S(2)}, u32[]{:S(2)}) collective-permute-start(bf16[48,1792]{1,0:T(8,128)(2,1)} %get-tuple-element.44), channel_id=1, source_target_pairs={{0,160},{16,176},{32,0},{48,16},{128,32},{144,48},{160,128},{176,1... | collective-permute-start | bytes 516104 | tf_op jit(solution)/shard_map/ppermute | solution.py:20
  37.3 13.7 %collective-permute-start.8 = (bf16[96,1792]{1,0:T(8,128)(2,1)}, bf16[96,1792]{1,0:T(8,128)(2,1)S(1)}, u32[]{:S(2)}, u32[]{:S(2)}) collective-permute-start(bf16[96,1792]{1,0:T(8,128)(2,1)} %get-tuple-element.29), channel_id=1, source_target_pairs={{0,176},{16,0},{32,16},{48,32},{128,48},{144,128},{160,144},{176,1... | collective-permute-start | bytes 1032200 | tf_op jit(solution)/shard_map/ppermute | solution.py:20
  38.5 12.6 %collective-permute-start.5 = (bf16[96,1792]{1,0:T(8,128)(2,1)S(1)}, bf16[96,1792]{1,0:T(8,128)(2,1)S(1)}, u32[]{:S(2)}, u32[]{:S(2)}) collective-permute-start(bf16[96,1792]{1,0:T(8,128)(2,1)S(1)} %get-tuple-element.30), channel_id=1, source_target_pairs={{0,16},{16,32},{32,48},{48,128},{128,144},{144,160},{160,176},{176... | collective-permute-start | bytes 1032200 | tf_op jit(solution)/shard_map/ppermute | solution.py:20
  53.5 32.6 %all-to-all-start.1 = ((bf16[16,24,1792]{2,1,0:T(8,128)(2,1)}), bf16[16,24,1792]{2,1,0:T(8,128)(2,1)S(1)}, u32[]{:S(2)}, u32[]{:S(2)}) async-start(bf16[16,24,1792]{2,1,0:T(8,128)(2,1)} %copy.86), calls=%async_computation.1 | async-start | bytes 2752512 | tf_op jit(solution)/shard_map/all_to_all | solution.py:24
  64.8 10.1 %collective-permute-start.3 = (bf16[48,1792]{1,0:T(8,128)(2,1)}, bf16[48,1792]{1,0:T(8,128)(2,1)}, u32[]{:S(2)}, u32[]{:S(2)}) collective-permute-start(bf16[48,1792]{1,0:T(8,128)(2,1)} %bitcast.101), channel_id=1, source_target_pairs={{0,160},{16,176},{32,0},{48,16},{128,32},{144,48},{160,128},{176,1... | collective-permute-start | bytes 516104 | tf_op jit(solution)/shard_map/ppermute | solution.py:20
  67.6 11.2 %collective-permute-start.2 = (bf16[48,1792]{1,0:T(8,128)(2,1)S(1)}, bf16[48,1792]{1,0:T(8,128)(2,1)}, u32[]{:S(2)}, u32[]{:S(2)}) collective-permute-start(bf16[48,1792]{1,0:T(8,128)(2,1)S(1)} %bitcast.122), channel_id=1, source_target_pairs={{0,32},{16,48},{32,128},{48,144},{128,160},{144,176},{160,0},{176,... | collective-permute-start | bytes 516104 | tf_op jit(solution)/shard_map/ppermute | solution.py:20
  68.1 14.1 %collective-permute-start.4 = (bf16[96,1792]{1,0:T(8,128)(2,1)S(1)}, bf16[96,1792]{1,0:T(8,128)(2,1)}, u32[]{:S(2)}, u32[]{:S(2)}) collective-permute-start(bf16[96,1792]{1,0:T(8,128)(2,1)S(1)} %squeeze.62), channel_id=1, source_target_pairs={{0,176},{16,0},{32,16},{48,32},{128,48},{144,128},{160,144},{176,1... | collective-permute-start | bytes 1032200 | tf_op jit(solution)/shard_map/ppermute | solution.py:20
  72.3 12.5 %collective-permute-start.1 = (bf16[96,1792]{1,0:T(8,128)(2,1)S(1)}, bf16[96,1792]{1,0:T(8,128)(2,1)}, u32[]{:S(2)}, u32[]{:S(2)}) collective-permute-start(bf16[96,1792]{1,0:T(8,128)(2,1)S(1)} %squeeze.59), channel_id=1, source_target_pairs={{0,16},{16,32},{32,48},{48,128},{128,144},{144,160},{160,176},{176... | collective-permute-start | bytes 1032200 | tf_op jit(solution)/shard_map/ppermute | solution.py:20
  87.9 5.4 %collective-permute-start.9 = (bf16[2,384,1792]{2,1,0:T(8,128)(2,1)}, bf16[2,384,1792]{2,1,0:T(8,128)(2,1)}, u32[]{:S(2)}, u32[]{:S(2)}) collective-permute-start(bf16[2,384,1792]{2,1,0:T(8,128)(2,1)} %pad_maximum_fusion), channel_id=1, source_target_pairs={{0,64},{64,0},{1,65},{65,1},{2,66},{66,2},{3,67},{67,3},{4,68},{68... | collective-permute-start | bytes 8257544 | tf_op jit(solution)/shard_map/ppermute | solution.py:15
  93.4 3.0 %slice-start = ((s8[7340032]{0:T(1024)(128)(4,1)}), s8[4194304]{0:T(1024)(128)(4,1)S(1)}, s32[]{:S(2)}) async-start(s8[7340032]{0:T(1024)(128)(4,1)} %bitcast.125), calls=%async_computation.4 | async-start | bytes 8388608
  95.5 2.1 %slice-start.1 = ((s8[7340032]{0:T(1024)(128)(4,1)}), s8[3145728]{0:T(1024)(128)(4,1)S(1)}, s32[]{:S(2)}) async-start(s8[7340032]{0:T(1024)(128)(4,1)} %bitcast.125), calls=%async_computation.5 | async-start | bytes 6291456
  97.6 3.3 %copy-start = (bf16[2,256,3584]{2,1,0:T(8,128)(2,1)S(1)}, bf16[2,256,3584]{2,1,0:T(8,128)(2,1)}, u32[]{:S(2)}) copy-start(bf16[2,256,3584]{2,1,0:T(8,128)(2,1)} %param.11) | copy-start | bytes 11010052
  104.0 5.2 %collective-permute-start.10 = (bf16[2,384,1792]{2,1,0:T(8,128)(2,1)S(1)}, bf16[2,384,1792]{2,1,0:T(8,128)(2,1)S(1)}, u32[]{:S(2)}, u32[]{:S(2)}) collective-permute-start(bf16[2,384,1792]{2,1,0:T(8,128)(2,1)S(1)} %broadcast_select_fusion), channel_id=1, source_target_pairs={{0,64},{64,0},{1,65},{65,1},{2,66},{66,2},{3,67},{67,3},{4,68},{68... | collective-permute-start | bytes 8257544 | tf_op jit(solution)/shard_map/ppermute | solution.py:15
  112.0 30.7 %all-to-all-start.3 = ((bf16[16,24,1792]{2,1,0:T(8,128)(2,1)}), bf16[16,24,1792]{2,1,0:T(8,128)(2,1)}, u32[]{:S(2)}, u32[]{:S(2)}) async-start(bf16[16,24,1792]{2,1,0:T(8,128)(2,1)} %bitcast.112), calls=%async_computation.3 | async-start | bytes 2752512 | tf_op jit(solution)/shard_map/all_to_all | solution.py:24
  121.0 10.0 %collective-permute-start.12 = (bf16[48,1792]{1,0:T(8,128)(2,1)}, bf16[48,1792]{1,0:T(8,128)(2,1)}, u32[]{:S(2)}, u32[]{:S(2)}) collective-permute-start(bf16[48,1792]{1,0:T(8,128)(2,1)} %get-tuple-element.31), channel_id=1, source_target_pairs={{0,160},{16,176},{32,0},{48,16},{128,32},{144,48},{160,128},{176,1... | collective-permute-start | bytes 516104 | tf_op jit(solution)/shard_map/ppermute | solution.py:20
  121.0 12.2 %collective-permute-start.13 = (bf16[48,1792]{1,0:T(8,128)(2,1)}, bf16[48,1792]{1,0:T(8,128)(2,1)}, u32[]{:S(2)}, u32[]{:S(2)}) collective-permute-start(bf16[48,1792]{1,0:T(8,128)(2,1)} %get-tuple-element.32), channel_id=1, source_target_pairs={{0,32},{16,48},{32,128},{48,144},{128,160},{144,176},{160,0},{176,... | collective-permute-start | bytes 516104 | tf_op jit(solution)/shard_map/ppermute | solution.py:20
  124.8 15.5 %collective-permute-start.14 = (bf16[96,1792]{1,0:T(8,128)(2,1)}, bf16[96,1792]{1,0:T(8,128)(2,1)S(1)}, u32[]{:S(2)}, u32[]{:S(2)}) collective-permute-start(bf16[96,1792]{1,0:T(8,128)(2,1)} %get-tuple-element.18), channel_id=1, source_target_pairs={{0,16},{16,32},{32,48},{48,128},{128,144},{144,160},{160,176},{176... | collective-permute-start | bytes 1032200 | tf_op jit(solution)/shard_map/ppermute | solution.py:20
  124.8 15.6 %collective-permute-start.11 = (bf16[96,1792]{1,0:T(8,128)(2,1)S(1)}, bf16[96,1792]{1,0:T(8,128)(2,1)S(1)}, u32[]{:S(2)}, u32[]{:S(2)}) collective-permute-start(bf16[96,1792]{1,0:T(8,128)(2,1)S(1)} %get-tuple-element.19), channel_id=1, source_target_pairs={{0,176},{16,0},{32,16},{48,32},{128,48},{144,128},{160,144},{176,1... | collective-permute-start | bytes 1032200 | tf_op jit(solution)/shard_map/ppermute | solution.py:20
  142.8 31.3 %all-to-all-start.2 = ((bf16[16,24,1792]{2,1,0:T(8,128)(2,1)}), bf16[16,24,1792]{2,1,0:T(8,128)(2,1)S(1)}, u32[]{:S(2)}, u32[]{:S(2)}) async-start(bf16[16,24,1792]{2,1,0:T(8,128)(2,1)} %copy.90), calls=%async_computation.2 | async-start | bytes 2752512 | tf_op jit(solution)/shard_map/all_to_all | solution.py:24
  154.8 11.4 %collective-permute-start.17 = (bf16[48,1792]{1,0:T(8,128)(2,1)}, bf16[48,1792]{1,0:T(8,128)(2,1)}, u32[]{:S(2)}, u32[]{:S(2)}) collective-permute-start(bf16[48,1792]{1,0:T(8,128)(2,1)} %bitcast.99), channel_id=1, source_target_pairs={{0,32},{16,48},{32,128},{48,144},{128,160},{144,176},{160,0},{176,... | collective-permute-start | bytes 516104 | tf_op jit(solution)/shard_map/ppermute | solution.py:20
  154.8 11.4 %collective-permute-start.16 = (bf16[48,1792]{1,0:T(8,128)(2,1)}, bf16[48,1792]{1,0:T(8,128)(2,1)}, u32[]{:S(2)}, u32[]{:S(2)}) collective-permute-start(bf16[48,1792]{1,0:T(8,128)(2,1)} %bitcast.100), channel_id=1, source_target_pairs={{0,160},{16,176},{32,0},{48,16},{128,32},{144,48},{160,128},{176,1... | collective-permute-start | bytes 516104 | tf_op jit(solution)/shard_map/ppermute | solution.py:20
  159.2 12.6 %collective-permute-start.18 = (bf16[96,1792]{1,0:T(8,128)(2,1)S(1)}, bf16[96,1792]{1,0:T(8,128)(2,1)S(1)}, u32[]{:S(2)}, u32[]{:S(2)}) collective-permute-start(bf16[96,1792]{1,0:T(8,128)(2,1)S(1)} %squeeze.74), channel_id=1, source_target_pairs={{0,16},{16,32},{32,48},{48,128},{128,144},{144,160},{160,176},{176... | collective-permute-start | bytes 1032200 | tf_op jit(solution)/shard_map/ppermute | solution.py:20
  160.1 12.7 %collective-permute-start.15 = (bf16[96,1792]{1,0:T(8,128)(2,1)S(1)}, bf16[96,1792]{1,0:T(8,128)(2,1)}, u32[]{:S(2)}, u32[]{:S(2)}) collective-permute-start(bf16[96,1792]{1,0:T(8,128)(2,1)S(1)} %squeeze.71), channel_id=1, source_target_pairs={{0,176},{16,0},{32,16},{48,32},{128,48},{144,128},{160,144},{176,1... | collective-permute-start | bytes 1032200 | tf_op jit(solution)/shard_map/ppermute | solution.py:20
  163.1 11.0 %copy-start.2 = (f32[64,768]{1,0:T(8,128)S(1)}, f32[64,768]{1,0:T(8,128)}, u32[]{:S(2)}) copy-start(f32[64,768]{1,0:T(8,128)} %select_reduce_fusion) | copy-start | bytes 589828
  171.8 1.0 copy-start.1
  175.6 11.1 %collective-permute-start.19 = (bf16[64,896]{1,0:T(8,128)(2,1)S(1)}, bf16[64,896]{1,0:T(8,128)(2,1)S(1)}, u32[]{:S(2)}, u32[]{:S(2)}) collective-permute-start(bf16[64,896]{1,0:T(8,128)(2,1)S(1)} %select_convert_fusion), channel_id=1, source_target_pairs={{0,128},{128,0},{1,129},{129,1},{2,130},{130,2},{3,131},{131,3},{4... | collective-permute-start | bytes 344072 | tf_op jit(solution)/shard_map/ppermute | solution.py:15

commit v3 on v1

--- a/solution.py
+++ b/solution.py
@@ -129,11 +129,10 @@
     first = plane_a2a(first.reshape(n_plane, half_rows // n_plane, wide))
     second = joined(ring_back(second.reshape(n_z, half_rows // n_z, wide)), (half_rows // n_z, wide), 0)
     returned = jnp.concatenate([first.reshape(half_rows, wide), second.reshape(half_rows, wide)])
-    weighted = jnp.dot(
-        mixing,
-        returned.astype(jnp.float32),
-        precision=lax.Precision.HIGHEST,
-        preferred_element_type=jnp.float32,
+    high = mixing.astype(jnp.bfloat16)
+    low = (mixing - high.astype(jnp.float32)).astype(jnp.bfloat16)
+    weighted = jnp.dot(high, returned, preferred_element_type=jnp.float32) + jnp.dot(
+        low, returned, preferred_element_type=jnp.float32
     )
     own, away = pick(half == 0, weighted[:, :width], weighted[:, width:])
     return (own + pair_swap(away.astype(jnp.bfloat16), "zh").astype(jnp.float32)).astype(jnp.bfloat16)

time: 183 us -> 183 us (level)
  no operation moved by 1% of the time
where the time goes in v3:
time: 183 us; the launch traced here: 182 us
  starting transfers between devices  69.9 us (38%)
  waiting for transfers between devices  57.4 us (31%)
  local copies, waits for them, and re-layouts  29.2 us (16%)
  other arithmetic  16.6 us (9%)
  matrix products  8.34 us (5%)
    ppermute x16, waiting for transfers between devices, ring_shift(): lax.ppermute(value, RING, [(i, (i + shift) % size) for i in range(size)])  39.7 us
    ppermute x16, starting transfers between devices, ring_shift(): lax.ppermute(value, RING, [(i, (i + shift) % size) for i in range(size)])  30.2 us
    all_to_all x4, starting transfers between devices, plane_a2a(): return lax.all_to_all(value, PLANE, 0, 0, tiled=True)  29.2 us
    ppermute x4, waiting for transfers between devices, pair_swap(): return lax.ppermute(value, axis, [(0, 1), (1, 0)])  17.6 us
    ppermute x4, starting transfers between devices, pair_swap(): return lax.ppermute(value, axis, [(0, 1), (1, 0)])  10.5 us
    another operation x6, other arithmetic, joined(): return jnp.stack([piece.reshape(shape) for piece in pieces], axis=axis)  5.43 us
    unnamed x18, local copies, waits for them, and re-layouts  5.21 us
    select_n x3, other arithmetic, pick(): return (jnp.where(flag, first, second), jnp.where(flag, second, first))  3.73 us
  transfers between devices with their start and end apart: 24, of which 18 were waited for; matrix products, arithmetic and copies ran while one was open for 18% of the time, Pallas kernels for 0%

profile of v3, /device:TPU:2, one launch (start us, length us, event | category | flops | bytes accessed | tf_op | source)
XLA Modules:
  0.0 181.8 jit_solution(490984262195264114)
XLA Ops:
  0.0 7.2 %collective-permute-start = (bf16[64,896]{1,0:T(8,128)(2,1)}, bf16[64,896]{1,0:T(8,128)(2,1)S(1)}, u32[]{:S(2)}, u32[]{:S(2)}) collective-permute-start(bf16[64,896]{1,0:T(8,128)(2,1)} %param.6), channel_id=1, source_target_pairs={{0,128},{128,0},{1,129},{129,1},{2,130},{130,2},{3,131},{131,3},{4... | collective-permute-start | bytes 344072 | tf_op jit(solution)/shard_map/ppermute | solution.py:15
  13.1 1.7 fusion.64
  14.8 7.5 %all-to-all-start = ((bf16[16,24,1792]{2,1,0:T(8,128)(2,1)}), bf16[16,24,1792]{2,1,0:T(8,128)(2,1)}, u32[]{:S(2)}, u32[]{:S(2)}) async-start(bf16[16,24,1792]{2,1,0:T(8,128)(2,1)} %bitcast.111), calls=%async_computation | async-start | bytes 2752512 | tf_op jit(solution)/shard_map/all_to_all | solution.py:24
  22.3 1.8 slice_bitcast_fusion.7
  24.1 3.6 %collective-permute-start.6 = (bf16[48,1792]{1,0:T(8,128)(2,1)}, bf16[48,1792]{1,0:T(8,128)(2,1)}, u32[]{:S(2)}, u32[]{:S(2)}) collective-permute-start(bf16[48,1792]{1,0:T(8,128)(2,1)} %get-tuple-element.37), channel_id=1, source_target_pairs={{0,32},{16,48},{32,128},{48,144},{128,160},{144,176},{160,0},{176,... | collective-permute-start | bytes 516104 | tf_op jit(solution)/shard_map/ppermute | solution.py:20
  27.7 2.8 %collective-permute-start.7 = (bf16[48,1792]{1,0:T(8,128)(2,1)}, bf16[48,1792]{1,0:T(8,128)(2,1)}, u32[]{:S(2)}, u32[]{:S(2)}) collective-permute-start(bf16[48,1792]{1,0:T(8,128)(2,1)} %get-tuple-element.38), channel_id=1, source_target_pairs={{0,160},{16,176},{32,0},{48,16},{128,32},{144,48},{160,128},{176,1... | collective-permute-start | bytes 516104 | tf_op jit(solution)/shard_map/ppermute | solution.py:20
  31.8 2.7 %collective-permute-start.8 = (bf16[96,1792]{1,0:T(8,128)(2,1)S(1)}, bf16[96,1792]{1,0:T(8,128)(2,1)S(1)}, u32[]{:S(2)}, u32[]{:S(2)}) collective-permute-start(bf16[96,1792]{1,0:T(8,128)(2,1)S(1)} %get-tuple-element.23), channel_id=1, source_target_pairs={{0,176},{16,0},{32,16},{48,32},{128,48},{144,128},{160,144},{176,1... | collective-permute-start | bytes 1032200 | tf_op jit(solution)/shard_map/ppermute | solution.py:20
  34.7 3.8 %collective-permute-done.6 = bf16[48,1792]{1,0:T(8,128)(2,1)} collective-permute-done((bf16[48,1792]{1,0:T(8,128)(2,1)}, bf16[48,1792]{1,0:T(8,128)(2,1)}, u32[]{:S(2)}, u32[]{:S(2)}) %collective-permute-start.6) | collective-permute-done | bytes 172064 | tf_op jit(solution)/shard_map/ppermute | solution.py:20
  39.6 4.3 %collective-permute-done.5 = bf16[96,1792]{1,0:T(8,128)(2,1)S(1)} collective-permute-done((bf16[96,1792]{1,0:T(8,128)(2,1)}, bf16[96,1792]{1,0:T(8,128)(2,1)S(1)}, u32[]{:S(2)}, u32[]{:S(2)}) %collective-permute-start.5) | collective-permute-done | bytes 344096 | tf_op jit(solution)/shard_map/ppermute | solution.py:20
  45.8 1.5 copy.86
  47.3 7.2 %all-to-all-start.1 = ((bf16[16,24,1792]{2,1,0:T(8,128)(2,1)}), bf16[16,24,1792]{2,1,0:T(8,128)(2,1)S(1)}, u32[]{:S(2)}, u32[]{:S(2)}) async-start(bf16[16,24,1792]{2,1,0:T(8,128)(2,1)} %copy.86), calls=%async_computation.1 | async-start | bytes 2752512 | tf_op jit(solution)/shard_map/all_to_all | solution.py:24
  54.6 1.6 copy.78
  58.6 1.1 collective-permute-start.2
  60.4 3.0 %collective-permute-start.3 = (bf16[48,1792]{1,0:T(8,128)(2,1)}, bf16[48,1792]{1,0:T(8,128)(2,1)}, u32[]{:S(2)}, u32[]{:S(2)}) collective-permute-start(bf16[48,1792]{1,0:T(8,128)(2,1)} %bitcast.100), channel_id=1, source_target_pairs={{0,160},{16,176},{32,0},{48,16},{128,32},{144,48},{160,128},{176,1... | collective-permute-start | bytes 516104 | tf_op jit(solution)/shard_map/ppermute | solution.py:20
  64.2 3.2 %collective-permute-start.4 = (bf16[96,1792]{1,0:T(8,128)(2,1)S(1)}, bf16[96,1792]{1,0:T(8,128)(2,1)}, u32[]{:S(2)}, u32[]{:S(2)}) collective-permute-start(bf16[96,1792]{1,0:T(8,128)(2,1)S(1)} %squeeze.62), channel_id=1, source_target_pairs={{0,176},{16,0},{32,16},{48,32},{128,48},{144,128},{160,144},{176,1... | collective-permute-start | bytes 1032200 | tf_op jit(solution)/shard_map/ppermute | solution.py:20
  67.6 3.8 %collective-permute-done.2 = bf16[48,1792]{1,0:T(8,128)(2,1)S(1)} collective-permute-done((bf16[48,1792]{1,0:T(8,128)(2,1)}, bf16[48,1792]{1,0:T(8,128)(2,1)S(1)}, u32[]{:S(2)}, u32[]{:S(2)}) %collective-permute-start.2) | collective-permute-done | bytes 172064 | tf_op jit(solution)/shard_map/ppermute | solution.py:20
  73.2 2.0 %collective-permute-done.1 = bf16[96,1792]{1,0:T(8,128)(2,1)} collective-permute-done((bf16[96,1792]{1,0:T(8,128)(2,1)S(1)}, bf16[96,1792]{1,0:T(8,128)(2,1)}, u32[]{:S(2)}, u32[]{:S(2)}) %collective-permute-start.1) | collective-permute-done | bytes 344096 | tf_op jit(solution)/shard_map/ppermute | solution.py:20
  75.2 1.5 collective-permute-done.4
  76.7 1.3 pad_maximum_fusion.8
  78.0 1.8 pad_maximum_fusion
  79.7 5.4 %collective-permute-done.9 = bf16[2,384,1792]{2,1,0:T(8,128)(2,1)} collective-permute-done((bf16[2,384,1792]{2,1,0:T(8,128)(2,1)}, bf16[2,384,1792]{2,1,0:T(8,128)(2,1)}, u32[]{:S(2)}, u32[]{:S(2)}) %collective-permute-start.9) | collective-permute-done | bytes 2752544 | tf_op jit(solution)/shard_map/ppermute | solution.py:15
  85.2 2.1 %broadcast_select_fusion.2 = (bf16[2,384,1792]{2,1,0:T(8,128)(2,1)S(1)}, bf16[2,384,1792]{2,1,0:T(8,128)(2,1)S(1)}) fusion(bf16[2,384,1792]{2,1,0:T(8,128)(2,1)} %collective-permute-done.9, pred[]{:T(512)S(6)} %eq.95, bf16[1,384,1792]{2,1,0:T(8,128)(2,1)S(1)} %bitcast.103, bf16[1,384,1792]{2,1,0:T(8,128)(2,1)S(1)} %bitcast.105), kind=kLoop, calls=%fused_computation.18 | loop fusion | flops 4128768 | bytes 11010049 | tf_op jit(solution)/shard_map/jit(_where)/select_n | solution.py:45
  88.2 1.2 slice-done.1
  89.4 3.3 %fusion = f32[2,384,2,256]{3,1,2,0:T(8,128)S(1)} fusion(bf16[2,3584,2,256]{3,2,1,0:T(2,128)(2,1)S(1)} %bitcast.126, bf16[2,384,896]{2,1,0:T(8,128)(2,1)S(1)} %get-tuple-element.43, bf16[2,384,896]{2,1,0:T(8,128)(2,1)S(1)} %get-tuple-element.17, bf16[2,384,896]{2,1,0:T(8,128)(2,1)S(1)} %get-tuple-element.44, bf16[2,384,896]{2,1,0:T(8,128)(2,1)S(1)} %get-tuple-element.16), kind=kOutput, calls=%fused_computation | convolution fusion | flops 2840592384 | bytes 14417920 | tf_op jit(solution)/shard_map/srd,sdgf->srgf/dot_general | solution.py:116
  92.7 1.6 convolution_convert_fusion
  96.0 5.0 %collective-permute-done.10 = bf16[2,384,1792]{2,1,0:T(8,128)(2,1)S(1)} collective-permute-done((bf16[2,384,1792]{2,1,0:T(8,128)(2,1)S(1)}, bf16[2,384,1792]{2,1,0:T(8,128)(2,1)S(1)}, u32[]{:S(2)}, u32[]{:S(2)}) %collective-permute-start.10) | collective-permute-done | bytes 2752544 | tf_op jit(solution)/shard_map/ppermute | solution.py:15
  101.0 1.1 add_convert_fusion
  102.1 1.7 fusion.61
  103.9 7.2 %all-to-all-start.3 = ((bf16[16,24,1792]{2,1,0:T(8,128)(2,1)}), bf16[16,24,1792]{2,1,0:T(8,128)(2,1)}, u32[]{:S(2)}, u32[]{:S(2)}) async-start(bf16[16,24,1792]{2,1,0:T(8,128)(2,1)} %bitcast.110), calls=%async_computation.3 | async-start | bytes 2752512 | tf_op jit(solution)/shard_map/all_to_all | solution.py:24
  111.1 1.8 slice_bitcast_fusion.5
  112.9 3.2 %collective-permute-start.12 = (bf16[48,1792]{1,0:T(8,128)(2,1)}, bf16[48,1792]{1,0:T(8,128)(2,1)}, u32[]{:S(2)}, u32[]{:S(2)}) collective-permute-start(bf16[48,1792]{1,0:T(8,128)(2,1)} %get-tuple-element.25), channel_id=1, source_target_pairs={{0,160},{16,176},{32,0},{48,16},{128,32},{144,48},{160,128},{176,1... | collective-permute-start | bytes 516104 | tf_op jit(solution)/shard_map/ppermute | solution.py:20
  116.9 4.7 %collective-permute-start.11 = (bf16[96,1792]{1,0:T(8,128)(2,1)}, bf16[96,1792]{1,0:T(8,128)(2,1)S(1)}, u32[]{:S(2)}, u32[]{:S(2)}) collective-permute-start(bf16[96,1792]{1,0:T(8,128)(2,1)} %get-tuple-element.13), channel_id=1, source_target_pairs={{0,176},{16,0},{32,16},{48,32},{128,48},{144,128},{160,144},{176,1... | collective-permute-start | bytes 1032200 | tf_op jit(solution)/shard_map/ppermute | solution.py:20
  121.9 2.7 %collective-permute-done.12 = bf16[48,1792]{1,0:T(8,128)(2,1)} collective-permute-done((bf16[48,1792]{1,0:T(8,128)(2,1)}, bf16[48,1792]{1,0:T(8,128)(2,1)}, u32[]{:S(2)}, u32[]{:S(2)}) %collective-permute-start.12) | collective-permute-done | bytes 172064 | tf_op jit(solution)/shard_map/ppermute | solution.py:20
  124.6 4.3 %collective-permute-done.13 = bf16[48,1792]{1,0:T(8,128)(2,1)} collective-permute-done((bf16[48,1792]{1,0:T(8,128)(2,1)}, bf16[48,1792]{1,0:T(8,128)(2,1)}, u32[]{:S(2)}, u32[]{:S(2)}) %collective-permute-start.13) | collective-permute-done | bytes 172064 | tf_op jit(solution)/shard_map/ppermute | solution.py:20
  130.0 1.9 %collective-permute-done.11 = bf16[96,1792]{1,0:T(8,128)(2,1)S(1)} collective-permute-done((bf16[96,1792]{1,0:T(8,128)(2,1)}, bf16[96,1792]{1,0:T(8,128)(2,1)S(1)}, u32[]{:S(2)}, u32[]{:S(2)}) %collective-permute-start.11) | collective-permute-done | bytes 344096 | tf_op jit(solution)/shard_map/ppermute | solution.py:20
  132.0 3.4 %collective-permute-done.14 = bf16[96,1792]{1,0:T(8,128)(2,1)S(1)} collective-permute-done((bf16[96,1792]{1,0:T(8,128)(2,1)S(1)}, bf16[96,1792]{1,0:T(8,128)(2,1)S(1)}, u32[]{:S(2)}, u32[]{:S(2)}) %collective-permute-start.14) | collective-permute-done | bytes 344096 | tf_op jit(solution)/shard_map/ppermute | solution.py:20
  136.2 1.5 copy.90
  137.8 7.2 %all-to-all-start.2 = ((bf16[16,24,1792]{2,1,0:T(8,128)(2,1)}), bf16[16,24,1792]{2,1,0:T(8,128)(2,1)S(1)}, u32[]{:S(2)}, u32[]{:S(2)}) async-start(bf16[16,24,1792]{2,1,0:T(8,128)(2,1)} %copy.90), calls=%async_computation.2 | async-start | bytes 2752512 | tf_op jit(solution)/shard_map/all_to_all | solution.py:24
  145.0 1.6 copy.91
  149.8 2.9 %collective-permute-start.17 = (bf16[48,1792]{1,0:T(8,128)(2,1)}, bf16[48,1792]{1,0:T(8,128)(2,1)}, u32[]{:S(2)}, u32[]{:S(2)}) collective-permute-start(bf16[48,1792]{1,0:T(8,128)(2,1)} %bitcast.98), channel_id=1, source_target_pairs={{0,32},{16,48},{32,128},{48,144},{128,160},{144,176},{160,0},{176,... | collective-permute-start | bytes 516104 | tf_op jit(solution)/shard_map/ppermute | solution.py:20
  153.0 1.2 collective-permute-start.15
  155.4 1.2 select_reduce_fusion
  158.0 2.9 %collective-permute-done.17 = bf16[48,1792]{1,0:T(8,128)(2,1)} collective-permute-done((bf16[48,1792]{1,0:T(8,128)(2,1)}, bf16[48,1792]{1,0:T(8,128)(2,1)}, u32[]{:S(2)}, u32[]{:S(2)}) %collective-permute-start.17) | collective-permute-done | bytes 172064 | tf_op jit(solution)/shard_map/ppermute | solution.py:20
  161.9 3.2 %collective-permute-done.15 = bf16[96,1792]{1,0:T(8,128)(2,1)S(1)} collective-permute-done((bf16[96,1792]{1,0:T(8,128)(2,1)S(1)}, bf16[96,1792]{1,0:T(8,128)(2,1)S(1)}, u32[]{:S(2)}, u32[]{:S(2)}) %collective-permute-start.15) | collective-permute-done | bytes 344096 | tf_op jit(solution)/shard_map/ppermute | solution.py:20
  165.1 3.1 %collective-permute-done.18 = bf16[96,1792]{1,0:T(8,128)(2,1)} collective-permute-done((bf16[96,1792]{1,0:T(8,128)(2,1)S(1)}, bf16[96,1792]{1,0:T(8,128)(2,1)}, u32[]{:S(2)}, u32[]{:S(2)}) %collective-permute-start.18) | collective-permute-done | bytes 344096 | tf_op jit(solution)/shard_map/ppermute | solution.py:20
  168.3 1.3 pad_maximum_fusion.9
  170.8 3.1 %collective-permute-start.19 = (bf16[64,896]{1,0:T(8,128)(2,1)S(1)}, bf16[64,896]{1,0:T(8,128)(2,1)S(1)}, u32[]{:S(2)}, u32[]{:S(2)}) collective-permute-start(bf16[64,896]{1,0:T(8,128)(2,1)S(1)} %select_convert_fusion), channel_id=1, source_target_pairs={{0,128},{128,0},{1,129},{129,1},{2,130},{130,2},{3,131},{131,3},{4... | collective-permute-start | bytes 344072 | tf_op jit(solution)/shard_map/ppermute | solution.py:15
  173.9 7.2 %collective-permute-done.19 = bf16[64,896]{1,0:T(8,128)(2,1)S(1)} collective-permute-done((bf16[64,896]{1,0:T(8,128)(2,1)S(1)}, bf16[64,896]{1,0:T(8,128)(2,1)S(1)}, u32[]{:S(2)}, u32[]{:S(2)}) %collective-permute-start.19) | collective-permute-done | bytes 114720 | tf_op jit(solution)/shard_map/ppermute | solution.py:15
  (92 shorter events, 30.9 us)
Async XLA Ops:
  0.0 11.3 %collective-permute-start = (bf16[64,896]{1,0:T(8,128)(2,1)}, bf16[64,896]{1,0:T(8,128)(2,1)S(1)}, u32[]{:S(2)}, u32[]{:S(2)}) collective-permute-start(bf16[64,896]{1,0:T(8,128)(2,1)} %param.6), channel_id=1, source_target_pairs={{0,128},{128,0},{1,129},{129,1},{2,130},{130,2},{3,131},{131,3},{4... | collective-permute-start | bytes 344072 | tf_op jit(solution)/shard_map/ppermute | solution.py:15
  14.8 32.5 %all-to-all-start = ((bf16[16,24,1792]{2,1,0:T(8,128)(2,1)}), bf16[16,24,1792]{2,1,0:T(8,128)(2,1)}, u32[]{:S(2)}, u32[]{:S(2)}) async-start(bf16[16,24,1792]{2,1,0:T(8,128)(2,1)} %bitcast.111), calls=%async_computation | async-start | bytes 2752512 | tf_op jit(solution)/shard_map/all_to_all | solution.py:24
  24.1 14.3 %collective-permute-start.6 = (bf16[48,1792]{1,0:T(8,128)(2,1)}, bf16[48,1792]{1,0:T(8,128)(2,1)}, u32[]{:S(2)}, u32[]{:S(2)}) collective-permute-start(bf16[48,1792]{1,0:T(8,128)(2,1)} %get-tuple-element.37), channel_id=1, source_target_pairs={{0,32},{16,48},{32,128},{48,144},{128,160},{144,176},{160,0},{176,... | collective-permute-start | bytes 516104 | tf_op jit(solution)/shard_map/ppermute | solution.py:20
  27.7 10.7 %collective-permute-start.7 = (bf16[48,1792]{1,0:T(8,128)(2,1)}, bf16[48,1792]{1,0:T(8,128)(2,1)}, u32[]{:S(2)}, u32[]{:S(2)}) collective-permute-start(bf16[48,1792]{1,0:T(8,128)(2,1)} %get-tuple-element.38), channel_id=1, source_target_pairs={{0,160},{16,176},{32,0},{48,16},{128,32},{144,48},{160,128},{176,1... | collective-permute-start | bytes 516104 | tf_op jit(solution)/shard_map/ppermute | solution.py:20
  31.3 12.5 %collective-permute-start.5 = (bf16[96,1792]{1,0:T(8,128)(2,1)}, bf16[96,1792]{1,0:T(8,128)(2,1)S(1)}, u32[]{:S(2)}, u32[]{:S(2)}) collective-permute-start(bf16[96,1792]{1,0:T(8,128)(2,1)} %get-tuple-element.24), channel_id=1, source_target_pairs={{0,16},{16,32},{32,48},{48,128},{128,144},{144,160},{160,176},{176... | collective-permute-start | bytes 1032200 | tf_op jit(solution)/shard_map/ppermute | solution.py:20
  31.8 13.2 %collective-permute-start.8 = (bf16[96,1792]{1,0:T(8,128)(2,1)S(1)}, bf16[96,1792]{1,0:T(8,128)(2,1)S(1)}, u32[]{:S(2)}, u32[]{:S(2)}) collective-permute-start(bf16[96,1792]{1,0:T(8,128)(2,1)S(1)} %get-tuple-element.23), channel_id=1, source_target_pairs={{0,176},{16,0},{32,16},{48,32},{128,48},{144,128},{160,144},{176,1... | collective-permute-start | bytes 1032200 | tf_op jit(solution)/shard_map/ppermute | solution.py:20
  47.3 30.6 %all-to-all-start.1 = ((bf16[16,24,1792]{2,1,0:T(8,128)(2,1)}), bf16[16,24,1792]{2,1,0:T(8,128)(2,1)S(1)}, u32[]{:S(2)}, u32[]{:S(2)}) async-start(bf16[16,24,1792]{2,1,0:T(8,128)(2,1)} %copy.86), calls=%async_computation.1 | async-start | bytes 2752512 | tf_op jit(solution)/shard_map/all_to_all | solution.py:24
  58.6 12.8 %collective-permute-start.2 = (bf16[48,1792]{1,0:T(8,128)(2,1)}, bf16[48,1792]{1,0:T(8,128)(2,1)S(1)}, u32[]{:S(2)}, u32[]{:S(2)}) collective-permute-start(bf16[48,1792]{1,0:T(8,128)(2,1)} %bitcast.101), channel_id=1, source_target_pairs={{0,32},{16,48},{32,128},{48,144},{128,160},{144,176},{160,0},{176,... | collective-permute-start | bytes 516104 | tf_op jit(solution)/shard_map/ppermute | solution.py:20
  60.4 11.9 %collective-permute-start.3 = (bf16[48,1792]{1,0:T(8,128)(2,1)}, bf16[48,1792]{1,0:T(8,128)(2,1)}, u32[]{:S(2)}, u32[]{:S(2)}) collective-permute-start(bf16[48,1792]{1,0:T(8,128)(2,1)} %bitcast.100), channel_id=1, source_target_pairs={{0,160},{16,176},{32,0},{48,16},{128,32},{144,48},{160,128},{176,1... | collective-permute-start | bytes 516104 | tf_op jit(solution)/shard_map/ppermute | solution.py:20
  63.8 11.4 %collective-permute-start.1 = (bf16[96,1792]{1,0:T(8,128)(2,1)S(1)}, bf16[96,1792]{1,0:T(8,128)(2,1)}, u32[]{:S(2)}, u32[]{:S(2)}) collective-permute-start(bf16[96,1792]{1,0:T(8,128)(2,1)S(1)} %squeeze.59), channel_id=1, source_target_pairs={{0,16},{16,32},{32,48},{48,128},{128,144},{144,160},{160,176},{176... | collective-permute-start | bytes 1032200 | tf_op jit(solution)/shard_map/ppermute | solution.py:20
  64.2 12.5 %collective-permute-start.4 = (bf16[96,1792]{1,0:T(8,128)(2,1)S(1)}, bf16[96,1792]{1,0:T(8,128)(2,1)}, u32[]{:S(2)}, u32[]{:S(2)}) collective-permute-start(bf16[96,1792]{1,0:T(8,128)(2,1)S(1)} %squeeze.62), channel_id=1, source_target_pairs={{0,176},{16,0},{32,16},{48,32},{128,48},{144,128},{160,144},{176,1... | collective-permute-start | bytes 1032200 | tf_op jit(solution)/shard_map/ppermute | solution.py:20
  79.7 5.4 %collective-permute-start.9 = (bf16[2,384,1792]{2,1,0:T(8,128)(2,1)}, bf16[2,384,1792]{2,1,0:T(8,128)(2,1)}, u32[]{:S(2)}, u32[]{:S(2)}) collective-permute-start(bf16[2,384,1792]{2,1,0:T(8,128)(2,1)} %pad_maximum_fusion), channel_id=1, source_target_pairs={{0,64},{64,0},{1,65},{65,1},{2,66},{66,2},{3,67},{67,3},{4,68},{68... | collective-permute-start | bytes 8257544 | tf_op jit(solution)/shard_map/ppermute | solution.py:15
  85.2 3.0 %slice-start = ((s8[7340032]{0:T(1024)(128)(4,1)}), s8[4194304]{0:T(1024)(128)(4,1)S(1)}, s32[]{:S(2)}) async-start(s8[7340032]{0:T(1024)(128)(4,1)} %bitcast.125), calls=%async_computation.4 | async-start | bytes 8388608
  87.3 2.1 %slice-start.1 = ((s8[7340032]{0:T(1024)(128)(4,1)}), s8[3145728]{0:T(1024)(128)(4,1)S(1)}, s32[]{:S(2)}) async-start(s8[7340032]{0:T(1024)(128)(4,1)} %bitcast.125), calls=%async_computation.5 | async-start | bytes 6291456
  89.4 3.3 %copy-start = (bf16[2,256,3584]{2,1,0:T(8,128)(2,1)S(1)}, bf16[2,256,3584]{2,1,0:T(8,128)(2,1)}, u32[]{:S(2)}) copy-start(bf16[2,256,3584]{2,1,0:T(8,128)(2,1)} %param.11) | copy-start | bytes 11010052
  95.8 5.2 %collective-permute-start.10 = (bf16[2,384,1792]{2,1,0:T(8,128)(2,1)S(1)}, bf16[2,384,1792]{2,1,0:T(8,128)(2,1)S(1)}, u32[]{:S(2)}, u32[]{:S(2)}) collective-permute-start(bf16[2,384,1792]{2,1,0:T(8,128)(2,1)S(1)} %broadcast_select_fusion), channel_id=1, source_target_pairs={{0,64},{64,0},{1,65},{65,1},{2,66},{66,2},{3,67},{67,3},{4,68},{68... | collective-permute-start | bytes 8257544 | tf_op jit(solution)/shard_map/ppermute | solution.py:15
  103.9 33.9 %all-to-all-start.3 = ((bf16[16,24,1792]{2,1,0:T(8,128)(2,1)}), bf16[16,24,1792]{2,1,0:T(8,128)(2,1)}, u32[]{:S(2)}, u32[]{:S(2)}) async-start(bf16[16,24,1792]{2,1,0:T(8,128)(2,1)} %bitcast.110), calls=%async_computation.3 | async-start | bytes 2752512 | tf_op jit(solution)/shard_map/all_to_all | solution.py:24
  111.1 10.6 %copy-start.3 = (f32[64,8]{0,1:T(8,128)S(1)}, f32[64,8]{0,1:T(8,128)}, u32[]{:S(2)}) copy-start(f32[64,8]{0,1:T(8,128)} %param.8) | copy-start | bytes 6148
  112.9 11.7 %collective-permute-start.12 = (bf16[48,1792]{1,0:T(8,128)(2,1)}, bf16[48,1792]{1,0:T(8,128)(2,1)}, u32[]{:S(2)}, u32[]{:S(2)}) collective-permute-start(bf16[48,1792]{1,0:T(8,128)(2,1)} %get-tuple-element.25), channel_id=1, source_target_pairs={{0,160},{16,176},{32,0},{48,16},{128,32},{144,48},{160,128},{176,1... | collective-permute-start | bytes 516104 | tf_op jit(solution)/shard_map/ppermute | solution.py:20
  116.1 12.7 %collective-permute-start.13 = (bf16[48,1792]{1,0:T(8,128)(2,1)}, bf16[48,1792]{1,0:T(8,128)(2,1)}, u32[]{:S(2)}, u32[]{:S(2)}) collective-permute-start(bf16[48,1792]{1,0:T(8,128)(2,1)} %get-tuple-element.26), channel_id=1, source_target_pairs={{0,32},{16,48},{32,128},{48,144},{128,160},{144,176},{160,0},{176,... | collective-permute-start | bytes 516104 | tf_op jit(solution)/shard_map/ppermute | solution.py:20
  116.9 15.0 %collective-permute-start.11 = (bf16[96,1792]{1,0:T(8,128)(2,1)}, bf16[96,1792]{1,0:T(8,128)(2,1)S(1)}, u32[]{:S(2)}, u32[]{:S(2)}) collective-permute-start(bf16[96,1792]{1,0:T(8,128)(2,1)} %get-tuple-element.13), channel_id=1, source_target_pairs={{0,176},{16,0},{32,16},{48,32},{128,48},{144,128},{160,144},{176,1... | collective-permute-start | bytes 1032200 | tf_op jit(solution)/shard_map/ppermute | solution.py:20
  121.6 13.8 %collective-permute-start.14 = (bf16[96,1792]{1,0:T(8,128)(2,1)S(1)}, bf16[96,1792]{1,0:T(8,128)(2,1)S(1)}, u32[]{:S(2)}, u32[]{:S(2)}) collective-permute-start(bf16[96,1792]{1,0:T(8,128)(2,1)S(1)} %get-tuple-element.12), channel_id=1, source_target_pairs={{0,16},{16,32},{32,48},{48,128},{128,144},{144,160},{160,176},{176... | collective-permute-start | bytes 1032200 | tf_op jit(solution)/shard_map/ppermute | solution.py:20
  137.8 31.7 %all-to-all-start.2 = ((bf16[16,24,1792]{2,1,0:T(8,128)(2,1)}), bf16[16,24,1792]{2,1,0:T(8,128)(2,1)S(1)}, u32[]{:S(2)}, u32[]{:S(2)}) async-start(bf16[16,24,1792]{2,1,0:T(8,128)(2,1)} %copy.90), calls=%async_computation.2 | async-start | bytes 2752512 | tf_op jit(solution)/shard_map/all_to_all | solution.py:24
  149.1 8.9 %collective-permute-start.16 = (bf16[48,1792]{1,0:T(8,128)(2,1)}, bf16[48,1792]{1,0:T(8,128)(2,1)}, u32[]{:S(2)}, u32[]{:S(2)}) collective-permute-start(bf16[48,1792]{1,0:T(8,128)(2,1)} %bitcast.99), channel_id=1, source_target_pairs={{0,160},{16,176},{32,0},{48,16},{128,32},{144,48},{160,128},{176,1... | collective-permute-start | bytes 516104 | tf_op jit(solution)/shard_map/ppermute | solution.py:20
  149.8 11.1 %collective-permute-start.17 = (bf16[48,1792]{1,0:T(8,128)(2,1)}, bf16[48,1792]{1,0:T(8,128)(2,1)}, u32[]{:S(2)}, u32[]{:S(2)}) collective-permute-start(bf16[48,1792]{1,0:T(8,128)(2,1)} %bitcast.98), channel_id=1, source_target_pairs={{0,32},{16,48},{32,128},{48,144},{128,160},{144,176},{160,0},{176,... | collective-permute-start | bytes 516104 | tf_op jit(solution)/shard_map/ppermute | solution.py:20
  153.0 12.1 %collective-permute-start.15 = (bf16[96,1792]{1,0:T(8,128)(2,1)S(1)}, bf16[96,1792]{1,0:T(8,128)(2,1)S(1)}, u32[]{:S(2)}, u32[]{:S(2)}) collective-permute-start(bf16[96,1792]{1,0:T(8,128)(2,1)S(1)} %squeeze.71), channel_id=1, source_target_pairs={{0,176},{16,0},{32,16},{48,32},{128,48},{144,128},{160,144},{176,1... | collective-permute-start | bytes 1032200 | tf_op jit(solution)/shard_map/ppermute | solution.py:20
  154.4 13.9 %collective-permute-start.18 = (bf16[96,1792]{1,0:T(8,128)(2,1)S(1)}, bf16[96,1792]{1,0:T(8,128)(2,1)}, u32[]{:S(2)}, u32[]{:S(2)}) collective-permute-start(bf16[96,1792]{1,0:T(8,128)(2,1)S(1)} %squeeze.74), channel_id=1, source_target_pairs={{0,16},{16,32},{32,48},{48,128},{128,144},{144,160},{160,176},{176... | collective-permute-start | bytes 1032200 | tf_op jit(solution)/shard_map/ppermute | solution.py:20
  156.9 12.7 %copy-start.2 = (f32[64,768]{1,0:T(8,128)S(1)}, f32[64,768]{1,0:T(8,128)}, u32[]{:S(2)}) copy-start(f32[64,768]{1,0:T(8,128)} %select_reduce_fusion) | copy-start | bytes 589828
  165.1 3.1 %copy-start.1 = (bf16[96,1792]{1,0:T(8,128)(2,1)}, bf16[96,1792]{1,0:T(8,128)(2,1)S(1)}, u32[]{:S(2)}) copy-start(bf16[96,1792]{1,0:T(8,128)(2,1)S(1)} %collective-permute-done.15) | copy-start | bytes 1032196
  170.8 10.3 %collective-permute-start.19 = (bf16[64,896]{1,0:T(8,128)(2,1)S(1)}, bf16[64,896]{1,0:T(8,128)(2,1)S(1)}, u32[]{:S(2)}, u32[]{:S(2)}) collective-permute-start(bf16[64,896]{1,0:T(8,128)(2,1)S(1)} %select_convert_fusion), channel_id=1, source_target_pairs={{0,128},{128,0},{1,129},{129,1},{2,130},{130,2},{3,131},{131,3},{4... | collective-permute-start | bytes 344072 | tf_op jit(solution)/shard_map/ppermute | solution.py:15

commit v4 on v1

--- a/solution.py
+++ b/solution.py
@@ -135,7 +135,8 @@
         precision=lax.Precision.HIGHEST,
         preferred_element_type=jnp.float32,
     )
-    own, away = pick(half == 0, weighted[:, :width], weighted[:, width:])
+    own = lax.dynamic_slice_in_dim(weighted, half * width, width, axis=1)
+    away = lax.dynamic_slice_in_dim(weighted, (1 - half) * width, width, axis=1)
     return (own + pair_swap(away.astype(jnp.bfloat16), "zh").astype(jnp.float32)).astype(jnp.bfloat16)
 
 

time: 183 us -> 184 us (level)
    unnamed x18 -> x16, local copies, waits for them, and re-layouts: 5.21 us -> 5.21 us
where the time goes in v4:
time: 184 us; the launch traced here: 183 us
  starting transfers between devices  69.9 us (38%)
  waiting for transfers between devices  57.4 us (31%)
  local copies, waits for them, and re-layouts  29.1 us (16%)
  other arithmetic  16.6 us (9%)
  matrix products  9.55 us (5%)
    ppermute x16, waiting for transfers between devices, ring_shift(): lax.ppermute(value, RING, [(i, (i + shift) % size) for i in range(size)])  39.8 us
    ppermute x16, starting transfers between devices, ring_shift(): lax.ppermute(value, RING, [(i, (i + shift) % size) for i in range(size)])  30.2 us
    all_to_all x4, starting transfers between devices, plane_a2a(): return lax.all_to_all(value, PLANE, 0, 0, tiled=True)  29.1 us
    ppermute x4, waiting for transfers between devices, pair_swap(): return lax.ppermute(value, axis, [(0, 1), (1, 0)])  17.6 us
    ppermute x4, starting transfers between devices, pair_swap(): return lax.ppermute(value, axis, [(0, 1), (1, 0)])  10.5 us
    another operation x6, other arithmetic, joined(): return jnp.stack([piece.reshape(shape) for piece in pieces], axis=axis)  5.43 us
    unnamed x16, local copies, waits for them, and re-layouts  5.21 us
    select_n x3, other arithmetic, pick(): return (jnp.where(flag, first, second), jnp.where(flag, second, first))  3.73 us
  transfers between devices with their start and end apart: 24, of which 18 were waited for; matrix products, arithmetic and copies ran while one was open for 18% of the time, Pallas kernels for 0%

profile of v4, /device:TPU:2, one launch (start us, length us, event | category | flops | bytes accessed | tf_op | source)
XLA Modules:
  0.0 183.0 jit_solution(632299698196155258)
XLA Ops:
  0.0 7.2 %collective-permute-start = (bf16[64,896]{1,0:T(8,128)(2,1)}, bf16[64,896]{1,0:T(8,128)(2,1)S(1)}, u32[]{:S(2)}, u32[]{:S(2)}) collective-permute-start(bf16[64,896]{1,0:T(8,128)(2,1)} %param.6), channel_id=1, source_target_pairs={{0,128},{128,0},{1,129},{129,1},{2,130},{130,2},{3,131},{131,3},{4... | collective-permute-start | bytes 344072 | tf_op jit(solution)/shard_map/ppermute | solution.py:15
  13.1 1.7 fusion.63
  14.8 7.5 %all-to-all-start = ((bf16[16,24,1792]{2,1,0:T(8,128)(2,1)}), bf16[16,24,1792]{2,1,0:T(8,128)(2,1)}, u32[]{:S(2)}, u32[]{:S(2)}) async-start(bf16[16,24,1792]{2,1,0:T(8,128)(2,1)} %bitcast.112), calls=%async_computation | async-start | bytes 2752512 | tf_op jit(solution)/shard_map/all_to_all | solution.py:24
  22.3 1.8 slice_bitcast_fusion.7
  24.1 3.6 %collective-permute-start.6 = (bf16[48,1792]{1,0:T(8,128)(2,1)}, bf16[48,1792]{1,0:T(8,128)(2,1)}, u32[]{:S(2)}, u32[]{:S(2)}) collective-permute-start(bf16[48,1792]{1,0:T(8,128)(2,1)} %get-tuple-element.37), channel_id=1, source_target_pairs={{0,32},{16,48},{32,128},{48,144},{128,160},{144,176},{160,0},{176,... | collective-permute-start | bytes 516104 | tf_op jit(solution)/shard_map/ppermute | solution.py:20
  27.7 2.8 %collective-permute-start.7 = (bf16[48,1792]{1,0:T(8,128)(2,1)}, bf16[48,1792]{1,0:T(8,128)(2,1)}, u32[]{:S(2)}, u32[]{:S(2)}) collective-permute-start(bf16[48,1792]{1,0:T(8,128)(2,1)} %get-tuple-element.38), channel_id=1, source_target_pairs={{0,160},{16,176},{32,0},{48,16},{128,32},{144,48},{160,128},{176,1... | collective-permute-start | bytes 516104 | tf_op jit(solution)/shard_map/ppermute | solution.py:20
  31.8 2.7 %collective-permute-start.8 = (bf16[96,1792]{1,0:T(8,128)(2,1)S(1)}, bf16[96,1792]{1,0:T(8,128)(2,1)S(1)}, u32[]{:S(2)}, u32[]{:S(2)}) collective-permute-start(bf16[96,1792]{1,0:T(8,128)(2,1)S(1)} %get-tuple-element.23), channel_id=1, source_target_pairs={{0,176},{16,0},{32,16},{48,32},{128,48},{144,128},{160,144},{176,1... | collective-permute-start | bytes 1032200 | tf_op jit(solution)/shard_map/ppermute | solution.py:20
  34.6 3.8 %collective-permute-done.6 = bf16[48,1792]{1,0:T(8,128)(2,1)} collective-permute-done((bf16[48,1792]{1,0:T(8,128)(2,1)}, bf16[48,1792]{1,0:T(8,128)(2,1)}, u32[]{:S(2)}, u32[]{:S(2)}) %collective-permute-start.6) | collective-permute-done | bytes 172064 | tf_op jit(solution)/shard_map/ppermute | solution.py:20
  39.6 4.3 %collective-permute-done.5 = bf16[96,1792]{1,0:T(8,128)(2,1)S(1)} collective-permute-done((bf16[96,1792]{1,0:T(8,128)(2,1)}, bf16[96,1792]{1,0:T(8,128)(2,1)S(1)}, u32[]{:S(2)}, u32[]{:S(2)}) %collective-permute-start.5) | collective-permute-done | bytes 344096 | tf_op jit(solution)/shard_map/ppermute | solution.py:20
  45.8 1.5 copy.86
  47.3 7.2 %all-to-all-start.1 = ((bf16[16,24,1792]{2,1,0:T(8,128)(2,1)}), bf16[16,24,1792]{2,1,0:T(8,128)(2,1)S(1)}, u32[]{:S(2)}, u32[]{:S(2)}) async-start(bf16[16,24,1792]{2,1,0:T(8,128)(2,1)} %copy.86), calls=%async_computation.1 | async-start | bytes 2752512 | tf_op jit(solution)/shard_map/all_to_all | solution.py:24
  54.5 1.6 copy.78
  60.4 3.0 %collective-permute-start.3 = (bf16[48,1792]{1,0:T(8,128)(2,1)}, bf16[48,1792]{1,0:T(8,128)(2,1)}, u32[]{:S(2)}, u32[]{:S(2)}) collective-permute-start(bf16[48,1792]{1,0:T(8,128)(2,1)} %bitcast.101), channel_id=1, source_target_pairs={{0,160},{16,176},{32,0},{48,16},{128,32},{144,48},{160,128},{176,1... | collective-permute-start | bytes 516104 | tf_op jit(solution)/shard_map/ppermute | solution.py:20
  64.1 3.2 %collective-permute-start.4 = (bf16[96,1792]{1,0:T(8,128)(2,1)S(1)}, bf16[96,1792]{1,0:T(8,128)(2,1)}, u32[]{:S(2)}, u32[]{:S(2)}) collective-permute-start(bf16[96,1792]{1,0:T(8,128)(2,1)S(1)} %squeeze.62), channel_id=1, source_target_pairs={{0,176},{16,0},{32,16},{48,32},{128,48},{144,128},{160,144},{176,1... | collective-permute-start | bytes 1032200 | tf_op jit(solution)/shard_map/ppermute | solution.py:20
  67.6 3.8 %collective-permute-done.2 = bf16[48,1792]{1,0:T(8,128)(2,1)S(1)} collective-permute-done((bf16[48,1792]{1,0:T(8,128)(2,1)}, bf16[48,1792]{1,0:T(8,128)(2,1)S(1)}, u32[]{:S(2)}, u32[]{:S(2)}) %collective-permute-start.2) | collective-permute-done | bytes 172064 | tf_op jit(solution)/shard_map/ppermute | solution.py:20
  73.2 2.0 %collective-permute-done.1 = bf16[96,1792]{1,0:T(8,128)(2,1)} collective-permute-done((bf16[96,1792]{1,0:T(8,128)(2,1)S(1)}, bf16[96,1792]{1,0:T(8,128)(2,1)}, u32[]{:S(2)}, u32[]{:S(2)}) %collective-permute-start.1) | collective-permute-done | bytes 344096 | tf_op jit(solution)/shard_map/ppermute | solution.py:20
  75.2 1.5 collective-permute-done.4
  76.7 1.3 pad_maximum_fusion.5
  78.0 1.8 pad_maximum_fusion
  79.7 5.4 %collective-permute-done.9 = bf16[2,384,1792]{2,1,0:T(8,128)(2,1)} collective-permute-done((bf16[2,384,1792]{2,1,0:T(8,128)(2,1)}, bf16[2,384,1792]{2,1,0:T(8,128)(2,1)}, u32[]{:S(2)}, u32[]{:S(2)}) %collective-permute-start.9) | collective-permute-done | bytes 2752544 | tf_op jit(solution)/shard_map/ppermute | solution.py:15
  85.2 2.1 %broadcast_select_fusion.2 = (bf16[2,384,1792]{2,1,0:T(8,128)(2,1)S(1)}, bf16[2,384,1792]{2,1,0:T(8,128)(2,1)S(1)}) fusion(bf16[2,384,1792]{2,1,0:T(8,128)(2,1)} %collective-permute-done.9, pred[]{:T(512)S(6)} %eq.93, bf16[1,384,1792]{2,1,0:T(8,128)(2,1)S(1)} %bitcast.104, bf16[1,384,1792]{2,1,0:T(8,128)(2,1)S(1)} %bitcast.106), kind=kLoop, calls=%fused_computation.21 | loop fusion | flops 4128768 | bytes 11010049 | tf_op jit(solution)/shard_map/jit(_where)/select_n | solution.py:45
  88.2 1.2 slice-done.1
  89.4 3.3 %fusion = f32[2,384,2,256]{3,1,2,0:T(8,128)S(1)} fusion(bf16[2,3584,2,256]{3,2,1,0:T(2,128)(2,1)S(1)} %bitcast.125, bf16[2,384,896]{2,1,0:T(8,128)(2,1)S(1)} %get-tuple-element.43, bf16[2,384,896]{2,1,0:T(8,128)(2,1)S(1)} %get-tuple-element.17, bf16[2,384,896]{2,1,0:T(8,128)(2,1)S(1)} %get-tuple-element.44, bf16[2,384,896]{2,1,0:T(8,128)(2,1)S(1)} %get-tuple-element.16), kind=kOutput, calls=%fused_computation | convolution fusion | flops 2840592384 | bytes 14417920 | tf_op jit(solution)/shard_map/srd,sdgf->srgf/dot_general | solution.py:116
  92.7 1.6 convolution_convert_fusion
  96.0 5.0 %collective-permute-done.10 = bf16[2,384,1792]{2,1,0:T(8,128)(2,1)S(1)} collective-permute-done((bf16[2,384,1792]{2,1,0:T(8,128)(2,1)S(1)}, bf16[2,384,1792]{2,1,0:T(8,128)(2,1)S(1)}, u32[]{:S(2)}, u32[]{:S(2)}) %collective-permute-start.10) | collective-permute-done | bytes 2752544 | tf_op jit(solution)/shard_map/ppermute | solution.py:15
  101.0 1.1 add_convert_fusion
  102.1 1.7 fusion.60
  103.9 7.2 %all-to-all-start.3 = ((bf16[16,24,1792]{2,1,0:T(8,128)(2,1)}), bf16[16,24,1792]{2,1,0:T(8,128)(2,1)}, u32[]{:S(2)}, u32[]{:S(2)}) async-start(bf16[16,24,1792]{2,1,0:T(8,128)(2,1)} %bitcast.111), calls=%async_computation.3 | async-start | bytes 2752512 | tf_op jit(solution)/shard_map/all_to_all | solution.py:24
  111.1 1.8 slice_bitcast_fusion.5
  112.8 3.2 %collective-permute-start.12 = (bf16[48,1792]{1,0:T(8,128)(2,1)}, bf16[48,1792]{1,0:T(8,128)(2,1)}, u32[]{:S(2)}, u32[]{:S(2)}) collective-permute-start(bf16[48,1792]{1,0:T(8,128)(2,1)} %get-tuple-element.25), channel_id=1, source_target_pairs={{0,160},{16,176},{32,0},{48,16},{128,32},{144,48},{160,128},{176,1... | collective-permute-start | bytes 516104 | tf_op jit(solution)/shard_map/ppermute | solution.py:20
  116.9 4.7 %collective-permute-start.11 = (bf16[96,1792]{1,0:T(8,128)(2,1)}, bf16[96,1792]{1,0:T(8,128)(2,1)S(1)}, u32[]{:S(2)}, u32[]{:S(2)}) collective-permute-start(bf16[96,1792]{1,0:T(8,128)(2,1)} %get-tuple-element.13), channel_id=1, source_target_pairs={{0,176},{16,0},{32,16},{48,32},{128,48},{144,128},{160,144},{176,1... | collective-permute-start | bytes 1032200 | tf_op jit(solution)/shard_map/ppermute | solution.py:20
  121.8 2.7 %collective-permute-done.12 = bf16[48,1792]{1,0:T(8,128)(2,1)} collective-permute-done((bf16[48,1792]{1,0:T(8,128)(2,1)}, bf16[48,1792]{1,0:T(8,128)(2,1)}, u32[]{:S(2)}, u32[]{:S(2)}) %collective-permute-start.12) | collective-permute-done | bytes 172064 | tf_op jit(solution)/shard_map/ppermute | solution.py:20
  124.5 4.3 %collective-permute-done.13 = bf16[48,1792]{1,0:T(8,128)(2,1)} collective-permute-done((bf16[48,1792]{1,0:T(8,128)(2,1)}, bf16[48,1792]{1,0:T(8,128)(2,1)}, u32[]{:S(2)}, u32[]{:S(2)}) %collective-permute-start.13) | collective-permute-done | bytes 172064 | tf_op jit(solution)/shard_map/ppermute | solution.py:20
  129.9 1.9 %collective-permute-done.11 = bf16[96,1792]{1,0:T(8,128)(2,1)S(1)} collective-permute-done((bf16[96,1792]{1,0:T(8,128)(2,1)}, bf16[96,1792]{1,0:T(8,128)(2,1)S(1)}, u32[]{:S(2)}, u32[]{:S(2)}) %collective-permute-start.11) | collective-permute-done | bytes 344096 | tf_op jit(solution)/shard_map/ppermute | solution.py:20
  131.9 3.4 %collective-permute-done.14 = bf16[96,1792]{1,0:T(8,128)(2,1)S(1)} collective-permute-done((bf16[96,1792]{1,0:T(8,128)(2,1)S(1)}, bf16[96,1792]{1,0:T(8,128)(2,1)S(1)}, u32[]{:S(2)}, u32[]{:S(2)}) %collective-permute-start.14) | collective-permute-done | bytes 344096 | tf_op jit(solution)/shard_map/ppermute | solution.py:20
  136.2 1.5 copy.90
  137.7 7.2 %all-to-all-start.2 = ((bf16[16,24,1792]{2,1,0:T(8,128)(2,1)}), bf16[16,24,1792]{2,1,0:T(8,128)(2,1)S(1)}, u32[]{:S(2)}, u32[]{:S(2)}) async-start(bf16[16,24,1792]{2,1,0:T(8,128)(2,1)} %copy.90), calls=%async_computation.2 | async-start | bytes 2752512 | tf_op jit(solution)/shard_map/all_to_all | solution.py:24
  145.0 1.6 copy.91
  149.7 2.9 %collective-permute-start.17 = (bf16[48,1792]{1,0:T(8,128)(2,1)}, bf16[48,1792]{1,0:T(8,128)(2,1)}, u32[]{:S(2)}, u32[]{:S(2)}) collective-permute-start(bf16[48,1792]{1,0:T(8,128)(2,1)} %bitcast.99), channel_id=1, source_target_pairs={{0,32},{16,48},{32,128},{48,144},{128,160},{144,176},{160,0},{176,... | collective-permute-start | bytes 516104 | tf_op jit(solution)/shard_map/ppermute | solution.py:20
  153.0 1.1 collective-permute-start.15
  155.4 1.2 select_reduce_fusion
  157.9 2.9 %collective-permute-done.17 = bf16[48,1792]{1,0:T(8,128)(2,1)} collective-permute-done((bf16[48,1792]{1,0:T(8,128)(2,1)}, bf16[48,1792]{1,0:T(8,128)(2,1)}, u32[]{:S(2)}, u32[]{:S(2)}) %collective-permute-start.17) | collective-permute-done | bytes 172064 | tf_op jit(solution)/shard_map/ppermute | solution.py:20
  161.9 3.2 %collective-permute-done.15 = bf16[96,1792]{1,0:T(8,128)(2,1)S(1)} collective-permute-done((bf16[96,1792]{1,0:T(8,128)(2,1)S(1)}, bf16[96,1792]{1,0:T(8,128)(2,1)S(1)}, u32[]{:S(2)}, u32[]{:S(2)}) %collective-permute-start.15) | collective-permute-done | bytes 344096 | tf_op jit(solution)/shard_map/ppermute | solution.py:20
  165.1 3.1 %collective-permute-done.18 = bf16[96,1792]{1,0:T(8,128)(2,1)} collective-permute-done((bf16[96,1792]{1,0:T(8,128)(2,1)S(1)}, bf16[96,1792]{1,0:T(8,128)(2,1)}, u32[]{:S(2)}, u32[]{:S(2)}) %collective-permute-start.18) | collective-permute-done | bytes 344096 | tf_op jit(solution)/shard_map/ppermute | solution.py:20
  168.2 1.3 pad_maximum_fusion.6
  169.5 2.4 %fusion.8 = f32[64,1792]{1,0:T(8,128)S(1)} fusion(f32[64,768]{1,0:T(8,128)} %select_reduce_fusion, bf16[384,1792]{1,0:T(8,128)(2,1)S(1)} %bitcast.120, bf16[384,1792]{1,0:T(8,128)(2,1)S(1)} %bitcast.119), kind=kOutput, calls=%fused_computation.15 | convolution fusion | flops 1062469632 | bytes 3407872 | tf_op jit(solution)/shard_map/dot_general | solution.py:132
  172.0 3.1 %collective-permute-start.19 = (bf16[64,896]{1,0:T(8,128)(2,1)S(1)}, bf16[64,896]{1,0:T(8,128)(2,1)S(1)}, u32[]{:S(2)}, u32[]{:S(2)}) collective-permute-start(bf16[64,896]{1,0:T(8,128)(2,1)S(1)} %dynamic-slice_convert_fusion), channel_id=1, source_target_pairs={{0,128},{128,0},{1,129},{129,1},{2,130},{130,2},{3,131},{131,3},{4... | collective-permute-start | bytes 344072 | tf_op jit(solution)/shard_map/ppermute | solution.py:15
  175.1 7.2 %collective-permute-done.19 = bf16[64,896]{1,0:T(8,128)(2,1)S(1)} collective-permute-done((bf16[64,896]{1,0:T(8,128)(2,1)S(1)}, bf16[64,896]{1,0:T(8,128)(2,1)S(1)}, u32[]{:S(2)}, u32[]{:S(2)}) %collective-permute-start.19) | collective-permute-done | bytes 114720 | tf_op jit(solution)/shard_map/ppermute | solution.py:15
  (89 shorter events, 30.7 us)
Async XLA Ops:
  0.0 11.3 %collective-permute-start = (bf16[64,896]{1,0:T(8,128)(2,1)}, bf16[64,896]{1,0:T(8,128)(2,1)S(1)}, u32[]{:S(2)}, u32[]{:S(2)}) collective-permute-start(bf16[64,896]{1,0:T(8,128)(2,1)} %param.6), channel_id=1, source_target_pairs={{0,128},{128,0},{1,129},{129,1},{2,130},{130,2},{3,131},{131,3},{4... | collective-permute-start | bytes 344072 | tf_op jit(solution)/shard_map/ppermute | solution.py:15
  14.8 32.5 %all-to-all-start = ((bf16[16,24,1792]{2,1,0:T(8,128)(2,1)}), bf16[16,24,1792]{2,1,0:T(8,128)(2,1)}, u32[]{:S(2)}, u32[]{:S(2)}) async-start(bf16[16,24,1792]{2,1,0:T(8,128)(2,1)} %bitcast.112), calls=%async_computation | async-start | bytes 2752512 | tf_op jit(solution)/shard_map/all_to_all | solution.py:24
  24.1 14.3 %collective-permute-start.6 = (bf16[48,1792]{1,0:T(8,128)(2,1)}, bf16[48,1792]{1,0:T(8,128)(2,1)}, u32[]{:S(2)}, u32[]{:S(2)}) collective-permute-start(bf16[48,1792]{1,0:T(8,128)(2,1)} %get-tuple-element.37), channel_id=1, source_target_pairs={{0,32},{16,48},{32,128},{48,144},{128,160},{144,176},{160,0},{176,... | collective-permute-start | bytes 516104 | tf_op jit(solution)/shard_map/ppermute | solution.py:20
  27.7 10.7 %collective-permute-start.7 = (bf16[48,1792]{1,0:T(8,128)(2,1)}, bf16[48,1792]{1,0:T(8,128)(2,1)}, u32[]{:S(2)}, u32[]{:S(2)}) collective-permute-start(bf16[48,1792]{1,0:T(8,128)(2,1)} %get-tuple-element.38), channel_id=1, source_target_pairs={{0,160},{16,176},{32,0},{48,16},{128,32},{144,48},{160,128},{176,1... | collective-permute-start | bytes 516104 | tf_op jit(solution)/shard_map/ppermute | solution.py:20
  31.3 12.5 %collective-permute-start.5 = (bf16[96,1792]{1,0:T(8,128)(2,1)}, bf16[96,1792]{1,0:T(8,128)(2,1)S(1)}, u32[]{:S(2)}, u32[]{:S(2)}) collective-permute-start(bf16[96,1792]{1,0:T(8,128)(2,1)} %get-tuple-element.24), channel_id=1, source_target_pairs={{0,16},{16,32},{32,48},{48,128},{128,144},{144,160},{160,176},{176... | collective-permute-start | bytes 1032200 | tf_op jit(solution)/shard_map/ppermute | solution.py:20
  31.8 13.2 %collective-permute-start.8 = (bf16[96,1792]{1,0:T(8,128)(2,1)S(1)}, bf16[96,1792]{1,0:T(8,128)(2,1)S(1)}, u32[]{:S(2)}, u32[]{:S(2)}) collective-permute-start(bf16[96,1792]{1,0:T(8,128)(2,1)S(1)} %get-tuple-element.23), channel_id=1, source_target_pairs={{0,176},{16,0},{32,16},{48,32},{128,48},{144,128},{160,144},{176,1... | collective-permute-start | bytes 1032200 | tf_op jit(solution)/shard_map/ppermute | solution.py:20
  47.3 30.6 %all-to-all-start.1 = ((bf16[16,24,1792]{2,1,0:T(8,128)(2,1)}), bf16[16,24,1792]{2,1,0:T(8,128)(2,1)S(1)}, u32[]{:S(2)}, u32[]{:S(2)}) async-start(bf16[16,24,1792]{2,1,0:T(8,128)(2,1)} %copy.86), calls=%async_computation.1 | async-start | bytes 2752512 | tf_op jit(solution)/shard_map/all_to_all | solution.py:24
  58.6 12.9 %collective-permute-start.2 = (bf16[48,1792]{1,0:T(8,128)(2,1)}, bf16[48,1792]{1,0:T(8,128)(2,1)S(1)}, u32[]{:S(2)}, u32[]{:S(2)}) collective-permute-start(bf16[48,1792]{1,0:T(8,128)(2,1)} %bitcast.102), channel_id=1, source_target_pairs={{0,32},{16,48},{32,128},{48,144},{128,160},{144,176},{160,0},{176,... | collective-permute-start | bytes 516104 | tf_op jit(solution)/shard_map/ppermute | solution.py:20
  60.4 11.9 %collective-permute-start.3 = (bf16[48,1792]{1,0:T(8,128)(2,1)}, bf16[48,1792]{1,0:T(8,128)(2,1)}, u32[]{:S(2)}, u32[]{:S(2)}) collective-permute-start(bf16[48,1792]{1,0:T(8,128)(2,1)} %bitcast.101), channel_id=1, source_target_pairs={{0,160},{16,176},{32,0},{48,16},{128,32},{144,48},{160,128},{176,1... | collective-permute-start | bytes 516104 | tf_op jit(solution)/shard_map/ppermute | solution.py:20
  63.8 11.4 %collective-permute-start.1 = (bf16[96,1792]{1,0:T(8,128)(2,1)S(1)}, bf16[96,1792]{1,0:T(8,128)(2,1)}, u32[]{:S(2)}, u32[]{:S(2)}) collective-permute-start(bf16[96,1792]{1,0:T(8,128)(2,1)S(1)} %squeeze.59), channel_id=1, source_target_pairs={{0,16},{16,32},{32,48},{48,128},{128,144},{144,160},{160,176},{176... | collective-permute-start | bytes 1032200 | tf_op jit(solution)/shard_map/ppermute | solution.py:20
  64.1 12.5 %collective-permute-start.4 = (bf16[96,1792]{1,0:T(8,128)(2,1)S(1)}, bf16[96,1792]{1,0:T(8,128)(2,1)}, u32[]{:S(2)}, u32[]{:S(2)}) collective-permute-start(bf16[96,1792]{1,0:T(8,128)(2,1)S(1)} %squeeze.62), channel_id=1, source_target_pairs={{0,176},{16,0},{32,16},{48,32},{128,48},{144,128},{160,144},{176,1... | collective-permute-start | bytes 1032200 | tf_op jit(solution)/shard_map/ppermute | solution.py:20
  79.7 5.4 %collective-permute-start.9 = (bf16[2,384,1792]{2,1,0:T(8,128)(2,1)}, bf16[2,384,1792]{2,1,0:T(8,128)(2,1)}, u32[]{:S(2)}, u32[]{:S(2)}) collective-permute-start(bf16[2,384,1792]{2,1,0:T(8,128)(2,1)} %pad_maximum_fusion), channel_id=1, source_target_pairs={{0,64},{64,0},{1,65},{65,1},{2,66},{66,2},{3,67},{67,3},{4,68},{68... | collective-permute-start | bytes 8257544 | tf_op jit(solution)/shard_map/ppermute | solution.py:15
  85.2 3.0 %slice-start = ((s8[7340032]{0:T(1024)(128)(4,1)}), s8[4194304]{0:T(1024)(128)(4,1)S(1)}, s32[]{:S(2)}) async-start(s8[7340032]{0:T(1024)(128)(4,1)} %bitcast.124), calls=%async_computation.4 | async-start | bytes 8388608
  87.3 2.1 %slice-start.1 = ((s8[7340032]{0:T(1024)(128)(4,1)}), s8[3145728]{0:T(1024)(128)(4,1)S(1)}, s32[]{:S(2)}) async-start(s8[7340032]{0:T(1024)(128)(4,1)} %bitcast.124), calls=%async_computation.5 | async-start | bytes 6291456
  89.4 3.3 %copy-start = (bf16[2,256,3584]{2,1,0:T(8,128)(2,1)S(1)}, bf16[2,256,3584]{2,1,0:T(8,128)(2,1)}, u32[]{:S(2)}) copy-start(bf16[2,256,3584]{2,1,0:T(8,128)(2,1)} %param.11) | copy-start | bytes 11010052
  95.8 5.2 %collective-permute-start.10 = (bf16[2,384,1792]{2,1,0:T(8,128)(2,1)S(1)}, bf16[2,384,1792]{2,1,0:T(8,128)(2,1)S(1)}, u32[]{:S(2)}, u32[]{:S(2)}) collective-permute-start(bf16[2,384,1792]{2,1,0:T(8,128)(2,1)S(1)} %broadcast_select_fusion), channel_id=1, source_target_pairs={{0,64},{64,0},{1,65},{65,1},{2,66},{66,2},{3,67},{67,3},{4,68},{68... | collective-permute-start | bytes 8257544 | tf_op jit(solution)/shard_map/ppermute | solution.py:15
  103.9 33.9 %all-to-all-start.3 = ((bf16[16,24,1792]{2,1,0:T(8,128)(2,1)}), bf16[16,24,1792]{2,1,0:T(8,128)(2,1)}, u32[]{:S(2)}, u32[]{:S(2)}) async-start(bf16[16,24,1792]{2,1,0:T(8,128)(2,1)} %bitcast.111), calls=%async_computation.3 | async-start | bytes 2752512 | tf_op jit(solution)/shard_map/all_to_all | solution.py:24
  111.1 10.5 %copy-start.2 = (f32[64,8]{0,1:T(8,128)S(1)}, f32[64,8]{0,1:T(8,128)}, u32[]{:S(2)}) copy-start(f32[64,8]{0,1:T(8,128)} %param.8) | copy-start | bytes 6148
  112.8 11.6 %collective-permute-start.12 = (bf16[48,1792]{1,0:T(8,128)(2,1)}, bf16[48,1792]{1,0:T(8,128)(2,1)}, u32[]{:S(2)}, u32[]{:S(2)}) collective-permute-start(bf16[48,1792]{1,0:T(8,128)(2,1)} %get-tuple-element.25), channel_id=1, source_target_pairs={{0,160},{16,176},{32,0},{48,16},{128,32},{144,48},{160,128},{176,1... | collective-permute-start | bytes 516104 | tf_op jit(solution)/shard_map/ppermute | solution.py:20
  116.0 12.7 %collective-permute-start.13 = (bf16[48,1792]{1,0:T(8,128)(2,1)}, bf16[48,1792]{1,0:T(8,128)(2,1)}, u32[]{:S(2)}, u32[]{:S(2)}) collective-permute-start(bf16[48,1792]{1,0:T(8,128)(2,1)} %get-tuple-element.26), channel_id=1, source_target_pairs={{0,32},{16,48},{32,128},{48,144},{128,160},{144,176},{160,0},{176,... | collective-permute-start | bytes 516104 | tf_op jit(solution)/shard_map/ppermute | solution.py:20
  116.9 15.0 %collective-permute-start.11 = (bf16[96,1792]{1,0:T(8,128)(2,1)}, bf16[96,1792]{1,0:T(8,128)(2,1)S(1)}, u32[]{:S(2)}, u32[]{:S(2)}) collective-permute-start(bf16[96,1792]{1,0:T(8,128)(2,1)} %get-tuple-element.13), channel_id=1, source_target_pairs={{0,176},{16,0},{32,16},{48,32},{128,48},{144,128},{160,144},{176,1... | collective-permute-start | bytes 1032200 | tf_op jit(solution)/shard_map/ppermute | solution.py:20
  121.6 13.8 %collective-permute-start.14 = (bf16[96,1792]{1,0:T(8,128)(2,1)S(1)}, bf16[96,1792]{1,0:T(8,128)(2,1)S(1)}, u32[]{:S(2)}, u32[]{:S(2)}) collective-permute-start(bf16[96,1792]{1,0:T(8,128)(2,1)S(1)} %get-tuple-element.12), channel_id=1, source_target_pairs={{0,16},{16,32},{32,48},{48,128},{128,144},{144,160},{160,176},{176... | collective-permute-start | bytes 1032200 | tf_op jit(solution)/shard_map/ppermute | solution.py:20
  137.7 31.7 %all-to-all-start.2 = ((bf16[16,24,1792]{2,1,0:T(8,128)(2,1)}), bf16[16,24,1792]{2,1,0:T(8,128)(2,1)S(1)}, u32[]{:S(2)}, u32[]{:S(2)}) async-start(bf16[16,24,1792]{2,1,0:T(8,128)(2,1)} %copy.90), calls=%async_computation.2 | async-start | bytes 2752512 | tf_op jit(solution)/shard_map/all_to_all | solution.py:24
  149.1 8.9 %collective-permute-start.16 = (bf16[48,1792]{1,0:T(8,128)(2,1)}, bf16[48,1792]{1,0:T(8,128)(2,1)}, u32[]{:S(2)}, u32[]{:S(2)}) collective-permute-start(bf16[48,1792]{1,0:T(8,128)(2,1)} %bitcast.100), channel_id=1, source_target_pairs={{0,160},{16,176},{32,0},{48,16},{128,32},{144,48},{160,128},{176,1... | collective-permute-start | bytes 516104 | tf_op jit(solution)/shard_map/ppermute | solution.py:20
  149.7 11.1 %collective-permute-start.17 = (bf16[48,1792]{1,0:T(8,128)(2,1)}, bf16[48,1792]{1,0:T(8,128)(2,1)}, u32[]{:S(2)}, u32[]{:S(2)}) collective-permute-start(bf16[48,1792]{1,0:T(8,128)(2,1)} %bitcast.99), channel_id=1, source_target_pairs={{0,32},{16,48},{32,128},{48,144},{128,160},{144,176},{160,0},{176,... | collective-permute-start | bytes 516104 | tf_op jit(solution)/shard_map/ppermute | solution.py:20
  153.0 12.1 %collective-permute-start.15 = (bf16[96,1792]{1,0:T(8,128)(2,1)S(1)}, bf16[96,1792]{1,0:T(8,128)(2,1)S(1)}, u32[]{:S(2)}, u32[]{:S(2)}) collective-permute-start(bf16[96,1792]{1,0:T(8,128)(2,1)S(1)} %squeeze.71), channel_id=1, source_target_pairs={{0,176},{16,0},{32,16},{48,32},{128,48},{144,128},{160,144},{176,1... | collective-permute-start | bytes 1032200 | tf_op jit(solution)/shard_map/ppermute | solution.py:20
  154.4 13.9 %collective-permute-start.18 = (bf16[96,1792]{1,0:T(8,128)(2,1)S(1)}, bf16[96,1792]{1,0:T(8,128)(2,1)}, u32[]{:S(2)}, u32[]{:S(2)}) collective-permute-start(bf16[96,1792]{1,0:T(8,128)(2,1)S(1)} %squeeze.74), channel_id=1, source_target_pairs={{0,16},{16,32},{32,48},{48,128},{128,144},{144,160},{160,176},{176... | collective-permute-start | bytes 1032200 | tf_op jit(solution)/shard_map/ppermute | solution.py:20
  165.1 3.1 %copy-start.1 = (bf16[96,1792]{1,0:T(8,128)(2,1)}, bf16[96,1792]{1,0:T(8,128)(2,1)S(1)}, u32[]{:S(2)}) copy-start(bf16[96,1792]{1,0:T(8,128)(2,1)S(1)} %collective-permute-done.15) | copy-start | bytes 1032196
  172.0 10.3 %collective-permute-start.19 = (bf16[64,896]{1,0:T(8,128)(2,1)S(1)}, bf16[64,896]{1,0:T(8,128)(2,1)S(1)}, u32[]{:S(2)}, u32[]{:S(2)}) collective-permute-start(bf16[64,896]{1,0:T(8,128)(2,1)S(1)} %dynamic-slice_convert_fusion), channel_id=1, source_target_pairs={{0,128},{128,0},{1,129},{129,1},{2,130},{130,2},{3,131},{131,3},{4... | collective-permute-start | bytes 344072 | tf_op jit(solution)/shard_map/ppermute | solution.py:15
